TPU v7x, 512 devices: a whole 4x8x8 slice. The times are simulated.
512 devices in a mesh: dp: 8 (over z), cent: 64 (over x, y, core).
Axes of the slice: x: 4, y: 8, z: 8, core: 2. Of those that a mesh axis runs over, the one named last changes fastest.
Arguments:
- points: bfloat16 [24576, 1024], P(('dp', 'cent')), may hold values from -6 to 6
- assign: int32 [24576], P(('dp', 'cent')), may hold values from 0 to 32767, as said below
- centroids: float32 [32768, 1024], P('cent'), may hold values from -6 to 6
- counts: int32 [32768], P('cent'), may hold values from 1 to 4
Outputs:
- new_centroids: float32 [32768, 1024], P('cent')
- best: float32 [24576], P(('dp', 'cent'))
Inputs may be any that keep to these rules, and one draw needn't show every extreme that they name: `assign`: split the points into aligned blocks of 3072 points in order (the points of one dp index). In every block, the clusters k * 512 to (k + 1) * 512 - 1 receive exactly 48 points together, for every k.
All inputs are finite; a program needn't handle non-finite values.
Results may differ from a plain program's by a relative error of at most 0.0003.
Values may be sent and summed in bfloat16 or wider, within the bound.
No kernel may reach another device: no remote copies, remote signals or barrier semaphores. Data moves between devices by JAX's collectives and lax.ppermute only.
A program may use at most 128 MiB of HBM per device.

v0:
```python
import jax
import jax.numpy as jnp
from jax import lax
from jax.sharding import PartitionSpec as P


def renorm(merged):
    return merged * lax.rsqrt(jnp.mean(merged * merged, axis=1, keepdims=True) + 1e-05)


def cluster_terms(rows, labels, kdev):
    first = lax.axis_index("cent") * kdev
    local = labels - first
    onehot = (local[None, :] == jnp.arange(kdev, dtype=jnp.int32)[:, None]).astype(jnp.bfloat16)
    return jnp.dot(onehot, rows, preferred_element_type=jnp.float32)


def per_device(points, assign, centroids, counts):
    kdev = centroids.shape[0]
    pdev = points.shape[0]
    weighted = centroids * counts.astype(jnp.float32)[:, None]
    rows, labels = (
        lax.all_gather(points, "cent", axis=0, tiled=True),
        lax.all_gather(assign, "cent", axis=0, tiled=True),
    )
    sums = cluster_terms(rows, labels, kdev)
    total = lax.psum(sums, "dp")
    fresh = renorm(weighted + total)
    rounded = fresh.astype(jnp.bfloat16)
    scores = jnp.dot(rows, rounded.T, preferred_element_type=jnp.float32)
    local_best = jnp.max(scores, axis=1)
    merged_best = lax.pmax(local_best, "cent")
    top = lax.dynamic_slice_in_dim(merged_best, lax.axis_index("cent") * pdev, pdev, 0)
    values = points.astype(jnp.float32)
    width = points.shape[1]
    scale = width * jnp.sqrt(jnp.mean(values * values, axis=1) + 1e-06)
    return (fresh, top / scale)


def solution(mesh):
    placed = (P(("dp", "cent"), None), P(("dp", "cent")), P("cent", None), P("cent"))
    return jax.shard_map(
        per_device,
        mesh=mesh,
        in_specs=placed,
        out_specs=(P("cent", None), P(("dp", "cent"))),
        check_vma=False,
    )
```

profile of v0, /device:TPU:1, one launch (start us, length us, event | category | flops | bytes accessed | tf_op | source)
XLA Modules:
  0.0 614.7 jit_solution(2940238520247544569)
XLA Ops:
  7.2 0.0 all-gather.2.cloned.1.call-start
  7.2 0.7 all-gather.2.cloned.1.call-update
  7.9 0.0 all-reduce.3.cloned.1.call-start
  7.9 1.3 dynamic-slice
  9.9 0.9 dynamic-update-slice
  10.8 247.8 %all-reduce = s32[3072]{0:T(1024)S(1)} all-reduce(s32[3072]{0:T(1024)S(1)} %dynamic-update-slice), channel_id=1, replica_groups=mesh['dp'=8,'cent'=64] {'cent'}, use_global_device_ids=true, to_apply=%add | all-reduce | flops 3072 | bytes 24576
  258.6 0.0 all-gather.2.cloned.1.call-done
  258.6 0.0 copy-start.3
  258.6 7.5 %fusion = f32[512,1024]{1,0:T(8,128)} fusion(bf16[3072,1024]{1,0:T(8,128)(2,1)} %all-gather.2.cloned.1.call-done, s32[3072]{0:T(1024)S(1)} %broadcast_subtract_fusion), kind=kOutput, calls=%fused_computation.1 | convolution fusion | flops 3222798336 | bytes 8400896 | tf_op jit(solution)/shard_map/dot_general | solution.py:15
  266.1 0.0 copy-start.4
  266.1 0.0 copy-start
  266.1 0.0 all-reduce.3.cloned.1.call-update
  266.2 0.7 copy-done.4
  266.8 0.0 copy-done.3
  266.8 0.1 multiply_reduce_fusion.1
  266.9 85.3 %all-reduce.3.cloned.1.call-done = f32[512,1024]{1,0:T(8,128)} async-done(((f32[512,1024]{1,0:T(8,128)}), f32[512,1024]{1,0:T(8,128)}) %all-reduce.3.cloned.1.call-update) | async-done | bytes 2097168 | tf_op jit(solution)/shard_map/psum | solution.py:27
  352.3 0.0 copy-done
  352.3 0.0 copy-start.1
  352.3 2.2 multiply_reduce_fusion
  354.5 0.1 copy-done.1
  354.5 0.0 copy-start.5
  354.5 0.4 broadcast_multiply_fusion
  354.9 0.0 copy-start.2
  354.9 1.3 copy-done.2
  356.2 1.8 copy-done.5
  358.1 3.7 convolution_reduce_fusion
  361.8 245.5 %pmax.7 = f32[3072]{0:T(1024)S(1)} all-reduce(f32[3072]{0:T(1024)S(1)} %convolution_reduce_fusion), channel_id=1, replica_groups=mesh['dp'=8,'cent'=64] {'cent'}, use_global_device_ids=true, to_apply=%region_3.0 | all-reduce | flops 3072 | bytes 24576 | tf_op jit(solution)/shard_map/pmax | solution.py:32
  607.3 0.6 multiply_divide_fusion
  (4 shorter events, 0.0 us)
Async XLA Ops:
  7.2 251.4 %all-gather.2.cloned.1.call-start = ((), (), s32[]{:S(2)}) async-start(), calls=%async_computation | async-start | bytes 6389760 | tf_op jit(solution)/shard_map/all_gather | solution.py:23
  7.9 344.4 %all-reduce.3.cloned.1.call-start = ((), (), s32[]{:S(2)}) async-start(), calls=%async_computation.1 | async-start | bytes 4194304 | tf_op jit(solution)/shard_map/psum | solution.py:27
  258.6 8.2 %copy-start.3 = (bf16[48,1024]{1,0:T(8,128)(2,1)S(1)}, bf16[48,1024]{1,0:T(8,128)(2,1)}, u32[]{:S(2)}) copy-start(bf16[48,1024]{1,0:T(8,128)(2,1)} %param.4) | copy-start | bytes 294916
  266.1 0.7 copy-start.4
  266.1 86.2 %copy-start = (f32[512,1024]{1,0:T(8,128)S(1)}, f32[512,1024]{1,0:T(8,128)}, u32[]{:S(2)}) copy-start(f32[512,1024]{1,0:T(8,128)} %param.6) | copy-start | bytes 6291460
  352.3 2.2 copy-start.1
  354.5 3.5 copy-start.5
  354.9 1.3 copy-start.2
Sparse Core Ops, SparseCore 0:
  11.3 91.5 all-gather.1
  266.3 85.9 all-reduce.2
where the time goes:
time: 618 us; the launch traced here: 615 us
  blocking collectives  493 us (80%)
  waiting for transfers between devices  86 us (14%)
  between operations  14.7 us (2%)
  matrix products  11.2 us (2%)
    unnamed x1, blocking collectives  248 us
    pmax x1, blocking collectives, per_device(): merged_best = lax.pmax(local_best, 'cent')  246 us
    psum x1, waiting for transfers between devices, per_device(): total = lax.psum(sums, 'dp')  85.3 us
  transfers between devices with their start and end apart: 2, of which 1 were waited for; matrix products, arithmetic and copies ran while one was open for 0% of the time, Pallas kernels for 0%

commit v1 on v0

v1 whole, which is shorter than its diff:
```python
import jax
import jax.numpy as jnp
from jax import lax
from jax.sharding import PartitionSpec as P


def renorm(merged):
    return merged * lax.rsqrt(jnp.mean(merged * merged, axis=1, keepdims=True) + 1e-05)


def make_per_device(ncent):
    def per_device(points, assign, centroids, counts):
        kdev = centroids.shape[0]
        pdev, width = points.shape
        first = lax.axis_index("cent") * kdev
        weighted = centroids * counts.astype(jnp.float32)[:, None]

        rows = lax.all_gather(points, "cent", axis=0, tiled=True)
        labels = lax.all_to_all(
            jnp.broadcast_to(assign[None], (ncent, pdev)), "cent", 0, 0, tiled=True
        ).reshape(-1)

        local = labels - first
        mine = (local >= 0) & (local < kdev)
        rank = jnp.cumsum(mine.astype(jnp.int32)) - 1
        pick = mine[None, :] & (rank[None, :] == jnp.arange(pdev, dtype=jnp.int32)[:, None])
        picked = jnp.dot(pick.astype(jnp.bfloat16), rows, preferred_element_type=jnp.float32)
        picked_label = jnp.sum(jnp.where(pick, local[None, :], 0), axis=1)
        hi = (picked_label // 16).astype(jnp.bfloat16)
        lo = (picked_label % 16).astype(jnp.bfloat16)
        packed = jnp.concatenate(
            [picked.astype(jnp.bfloat16), hi[:, None], lo[:, None], jnp.zeros((pdev, 126), jnp.bfloat16)],
            axis=1,
        )

        gathered = lax.all_gather(packed, "dp", axis=0, tiled=True)
        grows = gathered[:, :width]
        glabel = gathered[:, width].astype(jnp.int32) * 16 + gathered[:, width + 1].astype(jnp.int32)
        onehot = (glabel[None, :] == jnp.arange(kdev, dtype=jnp.int32)[:, None]).astype(jnp.bfloat16)
        total = jnp.dot(onehot, grows, preferred_element_type=jnp.float32)

        fresh = renorm(weighted + total)
        rounded = fresh.astype(jnp.bfloat16)
        scores = jnp.dot(rows, rounded.T, preferred_element_type=jnp.float32)
        local_best = jnp.max(scores, axis=1)
        top = jnp.max(lax.all_to_all(local_best.reshape(ncent, pdev), "cent", 0, 0, tiled=True), axis=0)
        values = points.astype(jnp.float32)
        scale = width * jnp.sqrt(jnp.mean(values * values, axis=1) + 1e-06)
        return (fresh, top / scale)

    return per_device


def solution(mesh):
    placed = (P(("dp", "cent"), None), P(("dp", "cent")), P("cent", None), P("cent"))
    return jax.shard_map(
        make_per_device(mesh.shape["cent"]),
        mesh=mesh,
        in_specs=placed,
        out_specs=(P("cent", None), P(("dp", "cent"))),
        check_vma=False,
    )
```

time: 618 us -> 167 us (0.27)
  blocking collectives: 493 us -> 23.1 us
  starting transfers between devices: 0.08 us -> 22.7 us
    unnamed x1 -> x0, blocking collectives: 248 us -> none
    pmax x1 -> x0, blocking collectives: 246 us -> none  [per_device(): merged_best = lax.pmax(local_best, 'cent')]
    psum x1 -> x0, waiting for transfers between devices: 85.3 us -> none  [per_device(): total = lax.psum(sums, 'dp')]
    all_gather x1, waiting for transfers between devices: 0.01 us -> 71.6 us  [per_device(): rows = lax.all_gather(points, 'cent', axis=0, tiled=True)]
    all_gather x0 -> x1, blocking collectives: none -> 23.1 us  [per_device(): gathered = lax.all_gather(packed, 'dp', axis=0, tiled=True)]
    all_to_all x0 -> x2, starting transfers between devices: none -> 22.7 us  [the longest x1 11.6 us: per_device(): lax.all_to_all(jnp.broadcast_to(assign[None], (ncent, pdev)), 'cent', 0,...]
    all_to_all x0 -> x2, waiting for transfers between devices: none -> 17.7 us  [the longest x1 9.18 us: per_device(): lax.all_to_all(local_best.reshape(ncent, pdev), 'cent', 0, 0, tiled=True)]
  transfers between devices with their start and end apart: 2 -> 3, of which waited for: 1 -> 3; matrix products, arithmetic and copies ran while one was open for 0% -> 2% of each run, Pallas kernels for 0% -> 0%
where the time goes in v1:
time: 167 us
  waiting for transfers between devices  90 us (54%)
  blocking collectives  23.1 us (14%)
  starting transfers between devices  22.7 us (14%)
  between operations  14.1 us (8%)
  matrix products  10.4 us (6%)
  local copies, waits for them, and re-layouts  3.82 us (2%)
  other arithmetic  2.76 us (2%)
    all_gather x1, waiting for transfers between devices, per_device(): rows = lax.all_gather(points, 'cent', axis=0, tiled=True)  71.6 us
    all_gather x1, blocking collectives, per_device(): gathered = lax.all_gather(packed, 'dp', axis=0, tiled=True)  23.1 us
    all_to_all x1, starting transfers between devices, per_device(): lax.all_to_all(jnp.broadcast_to(assign[None], (ncent, pdev)), 'cent', 0,...  11.6 us
    all_to_all x1, starting transfers between devices, per_device(): lax.all_to_all(local_best.reshape(ncent, pdev), 'cent', 0, 0, tiled=True)  11.1 us
    all_to_all x1, waiting for transfers between devices, per_device(): lax.all_to_all(local_best.reshape(ncent, pdev), 'cent', 0, 0, tiled=True)  9.18 us
    all_to_all x1, waiting for transfers between devices, per_device(): lax.all_to_all(jnp.broadcast_to(assign[None], (ncent, pdev)), 'cent', 0,...  8.55 us
    dot_general x1, matrix products, per_device(): jnp.dot(pick.astype(jnp.bfloat16), rows, preferred_element_type=jnp.float32)  4.12 us
    dot_general x1, matrix products, per_device(): scores = jnp.dot(rows, rounded.T, preferred_element_type=jnp.float32)  3.75 us
  transfers between devices with their start and end apart: 3, of which 3 were waited for; matrix products, arithmetic and copies ran while one was open for 2% of the time, Pallas kernels for 0%

profile of v1, /device:TPU:1, one launch (start us, length us, event | category | flops | bytes accessed | tf_op | source)
XLA Modules:
  0.0 166.9 jit_solution(16707966086912412383)
XLA Ops:
  7.2 0.0 all-gather.2.cloned.1.call-start
  7.2 0.7 all-gather.2.cloned.1.call-update
  7.9 1.3 broadcast_in_dim.12
  9.2 11.6 %all-to-all-start = ((s32[64,1,48]{2,1,0:T(1,128)}), s32[64,1,48]{2,1,0:T(1,128)S(1)}, u32[]{:S(2)}, u32[]{:S(2)}) async-start(s32[64,1,48]{2,1,0:T(1,128)} %broadcast_in_dim.12), calls=%async_computation | async-start | bytes 65536 | tf_op jit(solution)/shard_map/all_to_all | solution.py:19
  20.8 0.7 convert_element_type.57
  21.5 8.5 %all-to-all-done = s32[64,1,48]{2,1,0:T(1,128)S(1)} async-done(((s32[64,1,48]{2,1,0:T(1,128)}), s32[64,1,48]{2,1,0:T(1,128)S(1)}, u32[]{:S(2)}, u32[]{:S(2)}) %all-to-all-start) | async-done | bytes 12320 | tf_op jit(solution)/shard_map/all_to_all | solution.py:19
  30.0 0.2 subtract_reduce_fusion
  30.2 0.1 reshape.173
  30.3 0.3 reduce-window.9
  30.6 0.1 slice.21
  30.7 0.1 sub.32
  30.8 0.1 slice_reduce_fusion
  30.9 0.1 add_bitcast_fusion
  31.0 0.2 select_reduce_fusion
  31.3 0.1 copy.19
  31.4 71.6 %all-gather.2.cloned.1.call-done = bf16[3072,1024]{1,0:T(8,128)(2,1)} async-done(((bf16[48,1024]{1,0:T(8,128)(2,1)}), bf16[3072,1024]{1,0:T(8,128)(2,1)}) %all-gather.2.cloned.1.call-update) | async-done | bytes 6291472 | tf_op jit(solution)/shard_map/all_gather | solution.py:18
  102.9 0.0 slice-start
  102.9 4.1 %convolution_convert_fusion = bf16[48,1024]{1,0:T(8,128)(2,1)S(1)} fusion(bf16[3072,1024]{1,0:T(8,128)(2,1)} %all-gather.2.cloned.1.call-done, s32[3072]{0:T(1024)S(1)} %add_bitcast_fusion, pred[3072]{0:T(1024)(128)(4,1)S(1)} %compare_and_fusion), kind=kOutput, calls=%fused_computation.3 | convolution fusion | flops 302333952 | bytes 6405120 | tf_op jit(solution)/shard_map/dot_general | solution.py:27
  107.1 0.1 concatenate.3
  107.2 23.1 %all_gather.7 = bf16[384,1152]{1,0:T(8,128)(2,1)S(1)} all-gather(bf16[48,1152]{1,0:T(8,128)(2,1)S(1)} %concatenate.3), channel_id=1, replica_groups=mesh['dp'=8,'cent'=64] {'dp'}, dimensions={0}, use_global_device_ids=true | all-gather | bytes 995328 | tf_op jit(solution)/shard_map/all_gather | solution.py:36
  130.2 0.2 add_reduce_fusion
  130.5 0.0 slice-start.1
  130.5 2.6 %multiply_reduce_fusion = (f32[512]{0:T(512)S(1)}, f32[512,1024]{1,0:T(8,128)S(1)}) fusion(bf16[384,1152]{1,0:T(8,128)(2,1)S(1)} %all_gather.7, s32[384]{0:T(512)S(1)} %add_reduce_fusion, f32[512,1024]{1,0:T(8,128)} %param.6, f32[512]{0:T(512)S(1)} %convert_element_type.57), kind=kOutput, calls=%fused_computation | convolution fusion | flops 404946432 | bytes 4986880 | tf_op jit(solution)/shard_map/dot_general | solution.py:40
  133.1 0.2 broadcast_multiply_fusion
  133.3 0.0 copy-start
  133.3 1.3 copy-done
  134.6 0.0 slice-done
  134.6 0.0 slice-done.1
  134.6 0.0 copy-start.1
  134.6 3.7 %convolution_reduce_fusion = f32[3072]{0:T(1024)S(1)} fusion(bf16[3072,1024]{1,0:T(8,128)(2,1)S(1)} %bitcast.7, f32[512,1024]{1,0:T(8,128)S(1)} %broadcast_multiply_fusion), kind=kOutput, calls=%fused_computation.2 | convolution fusion | flops 3223319552 | bytes 8400896 | tf_op jit(solution)/shard_map/dot_general | solution.py:44
  138.4 0.7 all_to_all.11
  139.0 11.1 %all-to-all-start.1 = ((f32[64,1,48]{2,1,0:T(1,128)}), f32[64,1,48]{2,1,0:T(1,128)S(1)}, u32[]{:S(2)}, u32[]{:S(2)}) async-start(f32[64,1,48]{2,1,0:T(1,128)} %bitcast.2), calls=%async_computation.1 | async-start | bytes 65536 | tf_op jit(solution)/shard_map/all_to_all | solution.py:46
  150.1 0.0 copy-done.1
  150.1 0.1 multiply_reduce_fusion.1
  150.3 9.2 %all-to-all-done.1 = f32[64,1,48]{2,1,0:T(1,128)S(1)} async-done(((f32[64,1,48]{2,1,0:T(1,128)}), f32[64,1,48]{2,1,0:T(1,128)S(1)}, u32[]{:S(2)}, u32[]{:S(2)}) %all-to-all-start.1) | async-done | bytes 12320 | tf_op jit(solution)/shard_map/all_to_all | solution.py:46
  159.4 0.1 reduce_max.19
  159.5 0.5 multiply_divide_fusion
  (6 shorter events, 0.1 us)
Async XLA Ops:
  7.2 95.8 %all-gather.2.cloned.1.call-start = ((), (), s32[]{:S(2)}) async-start(), calls=%async_computation.2 | async-start | bytes 6389760 | tf_op jit(solution)/shard_map/all_gather | solution.py:18
  9.2 20.9 %all-to-all-start = ((s32[64,1,48]{2,1,0:T(1,128)}), s32[64,1,48]{2,1,0:T(1,128)S(1)}, u32[]{:S(2)}, u32[]{:S(2)}) async-start(s32[64,1,48]{2,1,0:T(1,128)} %broadcast_in_dim.12), calls=%async_computation | async-start | bytes 65536 | tf_op jit(solution)/shard_map/all_to_all | solution.py:19
  102.9 31.7 %slice-start = ((s8[6291456]{0:T(1024)(128)(4,1)}), s8[2097152]{0:T(1024)(128)(4,1)S(1)}, s32[]{:S(2)}) async-start(s8[6291456]{0:T(1024)(128)(4,1)} %bitcast.6), calls=%async_computation.3 | async-start | bytes 4194304
  130.5 4.1 %slice-start.1 = ((s8[6291456]{0:T(1024)(128)(4,1)}), s8[4194304]{0:T(1024)(128)(4,1)S(1)}, s32[]{:S(2)}) async-start(s8[6291456]{0:T(1024)(128)(4,1)} %bitcast.6), calls=%async_computation.4 | async-start | bytes 8388608
  133.3 1.3 copy-start
  134.6 15.5 %copy-start.1 = (bf16[48,1024]{1,0:T(8,128)(2,1)S(1)}, bf16[48,1024]{1,0:T(8,128)(2,1)}, u32[]{:S(2)}) copy-start(bf16[48,1024]{1,0:T(8,128)(2,1)} %param.4) | copy-start | bytes 294916
  139.0 20.4 %all-to-all-start.1 = ((f32[64,1,48]{2,1,0:T(1,128)}), f32[64,1,48]{2,1,0:T(1,128)S(1)}, u32[]{:S(2)}, u32[]{:S(2)}) async-start(f32[64,1,48]{2,1,0:T(1,128)} %bitcast.2), calls=%async_computation.1 | async-start | bytes 65536 | tf_op jit(solution)/shard_map/all_to_all | solution.py:46
Sparse Core Ops, SparseCore 0:
  11.3 91.5 all-gather.1

commit v2 on v1

--- a/solution.py
+++ b/solution.py
@@ -24,8 +24,9 @@
         mine = (local >= 0) & (local < kdev)
         rank = jnp.cumsum(mine.astype(jnp.int32)) - 1
         pick = mine[None, :] & (rank[None, :] == jnp.arange(pdev, dtype=jnp.int32)[:, None])
-        picked = jnp.dot(pick.astype(jnp.bfloat16), rows, preferred_element_type=jnp.float32)
-        picked_label = jnp.sum(jnp.where(pick, local[None, :], 0), axis=1)
+        where = jnp.sum(jnp.where(pick, jnp.arange(rows.shape[0], dtype=jnp.int32)[None, :], 0), axis=1)
+        picked = jnp.take(rows, where, axis=0)
+        picked_label = jnp.take(local, where, axis=0)
         hi = (picked_label // 16).astype(jnp.bfloat16)
         lo = (picked_label % 16).astype(jnp.bfloat16)
         packed = jnp.concatenate(

time: 167 us -> 166 us (level)
  matrix products: 10.4 us -> 4.62 us
  local copies, waits for them, and re-layouts: 3.82 us -> 9.41 us
    gather x0 -> x3, local copies, waits for them, and re-layouts: none -> 5.2 us  [the longest x1 4.32 us: per_device(): picked = jnp.take(rows, where, axis=0)]
    dot_general x1 -> x0, matrix products: 4.12 us -> none  [per_device(): jnp.dot(pick.astype(jnp.bfloat16), rows, preferred_element_type=jnp.float32)]
    dot_general x1, matrix products: 2.57 us -> 0.85 us  [per_device(): total = jnp.dot(onehot, grows, preferred_element_type=jnp.float32)]
  transfers between devices with their start and end apart: 3 -> 3, of which waited for: 3 -> 3; matrix products, arithmetic and copies ran while one was open for 2% -> 3% of each run, Pallas kernels for 0% -> 0%
where the time goes in v2:
time: 166 us
  waiting for transfers between devices  88.9 us (54%)
  blocking collectives  23.1 us (14%)
  starting transfers between devices  22.7 us (14%)
  between operations  14.2 us (9%)
  local copies, waits for them, and re-layouts  9.41 us (6%)
  matrix products  4.62 us (3%)
  other arithmetic  2.96 us (2%)
    all_gather x1, waiting for transfers between devices, per_device(): rows = lax.all_gather(points, 'cent', axis=0, tiled=True)  70.5 us
    all_gather x1, blocking collectives, per_device(): gathered = lax.all_gather(packed, 'dp', axis=0, tiled=True)  23.1 us
    all_to_all x1, starting transfers between devices, per_device(): lax.all_to_all(jnp.broadcast_to(assign[None], (ncent, pdev)), 'cent', 0,...  11.6 us
    all_to_all x1, starting transfers between devices, per_device(): lax.all_to_all(local_best.reshape(ncent, pdev), 'cent', 0, 0, tiled=True)  11.1 us
    all_to_all x1, waiting for transfers between devices, per_device(): lax.all_to_all(local_best.reshape(ncent, pdev), 'cent', 0, 0, tiled=True)  9.18 us
    all_to_all x1, waiting for transfers between devices, per_device(): lax.all_to_all(jnp.broadcast_to(assign[None], (ncent, pdev)), 'cent', 0,...  8.55 us
    gather x1, local copies, waits for them, and re-layouts, per_device(): picked = jnp.take(rows, where, axis=0)  4.32 us
    dot_general x1, matrix products, per_device(): scores = jnp.dot(rows, rounded.T, preferred_element_type=jnp.float32)  3.76 us
  transfers between devices with their start and end apart: 3, of which 3 were waited for; matrix products, arithmetic and copies ran while one was open for 3% of the time, Pallas kernels for 0%

profile of v2, /device:TPU:1, one launch (start us, length us, event | category | flops | bytes accessed | tf_op | source)
XLA Modules:
  0.0 165.9 jit_solution(9390593339017220535)
XLA Ops:
  7.2 0.0 copy-start.1
  7.2 0.0 all-gather.2.cloned.1.call-start
  7.2 0.7 all-gather.2.cloned.1.call-update
  7.9 1.3 broadcast_in_dim.32
  9.2 11.6 %all-to-all-start = ((s32[64,1,48]{2,1,0:T(1,128)}), s32[64,1,48]{2,1,0:T(1,128)S(1)}, u32[]{:S(2)}, u32[]{:S(2)}) async-start(s32[64,1,48]{2,1,0:T(1,128)} %broadcast_in_dim.32), calls=%async_computation | async-start | bytes 65536 | tf_op jit(solution)/shard_map/all_to_all | solution.py:19
  20.8 0.7 convert_element_type.53
  21.5 8.5 %all-to-all-done = s32[64,1,48]{2,1,0:T(1,128)S(1)} async-done(((s32[64,1,48]{2,1,0:T(1,128)}), s32[64,1,48]{2,1,0:T(1,128)S(1)}, u32[]{:S(2)}, u32[]{:S(2)}) %all-to-all-start) | async-done | bytes 12320 | tf_op jit(solution)/shard_map/all_to_all | solution.py:19
  30.1 0.2 subtract_reduce_fusion
  30.3 0.1 reshape.208
  30.3 0.3 reduce-window.9
  30.6 0.1 slice.25
  30.7 0.1 sub.29
  30.8 0.1 slice_reduce_fusion
  31.0 0.1 add_bitcast_fusion
  31.0 0.2 select_reduce_fusion
  31.3 0.1 copy.19
  31.4 0.1 fusion.8
  31.5 0.8 gather_fusion.1
  32.3 0.1 copy.22
  32.4 70.5 %all-gather.2.cloned.1.call-done = bf16[3072,1024]{1,0:T(8,128)(2,1)} async-done(((bf16[48,1024]{1,0:T(8,128)(2,1)}), bf16[3072,1024]{1,0:T(8,128)(2,1)}) %all-gather.2.cloned.1.call-update) | async-done | bytes 6291472 | tf_op jit(solution)/shard_map/all_gather | solution.py:18
  103.0 4.3 %gather_fusion = bf16[48,1024]{1,0:T(8,128)(2,1)S(1)} fusion(bf16[3072,1024]{1,0:T(8,128)(2,1)} %all-gather.2.cloned.1.call-done, s32[1024]{0:T(1024)S(1)} %pad_clamp_fusion), kind=kCustom, calls=%fused_computation | custom fusion | bytes 196800 | tf_op jit(solution)/shard_map/jit(_take)/gather | solution.py:28
  107.3 0.1 broadcast_select_fusion
  107.4 0.1 concatenate.3
  107.5 23.1 %all_gather.7 = bf16[384,1152]{1,0:T(8,128)(2,1)S(1)} all-gather(bf16[48,1152]{1,0:T(8,128)(2,1)S(1)} %concatenate.3), channel_id=1, replica_groups=mesh['dp'=8,'cent'=64] {'dp'}, dimensions={0}, use_global_device_ids=true | all-gather | bytes 995328 | tf_op jit(solution)/shard_map/all_gather | solution.py:37
  130.5 0.2 add_reduce_fusion
  130.8 0.0 copy-done.1
  130.8 0.0 copy-start.3
  130.8 0.9 multiply_reduce_fusion
  131.6 0.2 broadcast_multiply_fusion
  131.9 1.7 %copy-done.3 = bf16[3072,1024]{1,0:T(8,128)(2,1)S(1)} copy-done((bf16[3072,1024]{1,0:T(8,128)(2,1)S(1)}, bf16[3072,1024]{1,0:T(8,128)(2,1)}, u32[]{:S(2)}) %copy-start.3) | copy-done | bytes 6291480
  133.6 0.0 copy-start
  133.6 0.0 copy-start.2
  133.6 3.8 %convolution_reduce_fusion = f32[3072]{0:T(1024)S(1)} fusion(bf16[3072,1024]{1,0:T(8,128)(2,1)S(1)} %copy-done.3, f32[512,1024]{1,0:T(8,128)S(1)} %broadcast_multiply_fusion), kind=kOutput, calls=%fused_computation.4 | convolution fusion | flops 3223319552 | bytes 8400896 | tf_op jit(solution)/shard_map/dot_general | solution.py:45
  137.3 0.0 copy-done
  137.3 0.7 all_to_all.11
  138.0 11.1 %all-to-all-start.1 = ((f32[64,1,48]{2,1,0:T(1,128)}), f32[64,1,48]{2,1,0:T(1,128)S(1)}, u32[]{:S(2)}, u32[]{:S(2)}) async-start(f32[64,1,48]{2,1,0:T(1,128)} %bitcast.3), calls=%async_computation.1 | async-start | bytes 65536 | tf_op jit(solution)/shard_map/all_to_all | solution.py:47
  149.1 0.0 copy-done.2
  149.1 0.1 multiply_reduce_fusion.1
  149.2 9.2 %all-to-all-done.1 = f32[64,1,48]{2,1,0:T(1,128)S(1)} async-done(((f32[64,1,48]{2,1,0:T(1,128)}), f32[64,1,48]{2,1,0:T(1,128)S(1)}, u32[]{:S(2)}, u32[]{:S(2)}) %all-to-all-start.1) | async-done | bytes 12320 | tf_op jit(solution)/shard_map/all_to_all | solution.py:47
  158.4 0.1 reduce_max.19
  158.5 0.5 multiply_divide_fusion
  (7 shorter events, 0.1 us)
Async XLA Ops:
  7.2 123.6 %copy-start.1 = (f32[512,1024]{1,0:T(8,128)S(1)}, f32[512,1024]{1,0:T(8,128)}, u32[]{:S(2)}) copy-start(f32[512,1024]{1,0:T(8,128)} %param.6) | copy-start | bytes 6291460
  7.2 95.8 %all-gather.2.cloned.1.call-start = ((), (), s32[]{:S(2)}) async-start(), calls=%async_computation.2 | async-start | bytes 6389760 | tf_op jit(solution)/shard_map/all_gather | solution.py:18
  9.2 20.9 %all-to-all-start = ((s32[64,1,48]{2,1,0:T(1,128)}), s32[64,1,48]{2,1,0:T(1,128)S(1)}, u32[]{:S(2)}, u32[]{:S(2)}) async-start(s32[64,1,48]{2,1,0:T(1,128)} %broadcast_in_dim.32), calls=%async_computation | async-start | bytes 65536 | tf_op jit(solution)/shard_map/all_to_all | solution.py:19
  130.8 2.8 %copy-start.3 = (bf16[3072,1024]{1,0:T(8,128)(2,1)S(1)}, bf16[3072,1024]{1,0:T(8,128)(2,1)}, u32[]{:S(2)}) copy-start(bf16[3072,1024]{1,0:T(8,128)(2,1)} %all-gather.2.cloned.1.call-done) | copy-start | bytes 18874372
  133.6 3.8 %copy-start = (f32[512,1024]{1,0:T(8,128)}, f32[512,1024]{1,0:T(8,128)S(1)}, u32[]{:S(2)}) copy-start(f32[512,1024]{1,0:T(8,128)S(1)} %broadcast_multiply_fusion) | copy-start | bytes 6291460
  133.6 15.5 %copy-start.2 = (bf16[48,1024]{1,0:T(8,128)(2,1)S(1)}, bf16[48,1024]{1,0:T(8,128)(2,1)}, u32[]{:S(2)}) copy-start(bf16[48,1024]{1,0:T(8,128)(2,1)} %param.4) | copy-start | bytes 294916
  138.0 20.4 %all-to-all-start.1 = ((f32[64,1,48]{2,1,0:T(1,128)}), f32[64,1,48]{2,1,0:T(1,128)S(1)}, u32[]{:S(2)}, u32[]{:S(2)}) async-start(f32[64,1,48]{2,1,0:T(1,128)} %bitcast.3), calls=%async_computation.1 | async-start | bytes 65536 | tf_op jit(solution)/shard_map/all_to_all | solution.py:47
Sparse Core Ops, SparseCore 0:
  11.3 91.5 all-gather.1

commit v3 on v2

--- a/solution.py
+++ b/solution.py
@@ -25,7 +25,7 @@
         rank = jnp.cumsum(mine.astype(jnp.int32)) - 1
         pick = mine[None, :] & (rank[None, :] == jnp.arange(pdev, dtype=jnp.int32)[:, None])
         where = jnp.sum(jnp.where(pick, jnp.arange(rows.shape[0], dtype=jnp.int32)[None, :], 0), axis=1)
-        picked = jnp.take(rows, where, axis=0)
+        picked = jnp.concatenate([lax.dynamic_slice_in_dim(rows, where[r], 1, 0) for r in range(pdev)], axis=0)
         picked_label = jnp.take(local, where, axis=0)
         hi = (picked_label // 16).astype(jnp.bfloat16)
         lo = (picked_label % 16).astype(jnp.bfloat16)

time: 166 us -> 192 us (1.16); the launches traced: 166 us -> 190 us
  between operations: 14.2 us -> 104 us
  waiting for transfers between devices: 88.9 us -> 18.5 us
  blocking collectives: 23.1 us -> 27.5 us
    all_gather x1, waiting for transfers between devices: 70.5 us -> 0.02 us  [per_device(): rows = lax.all_gather(points, 'cent', axis=0, tiled=True)]
    all_gather x1, blocking collectives: 23.1 us -> 27.5 us  [per_device(): gathered = lax.all_gather(packed, 'dp', axis=0, tiled=True)]
    gather x1 -> x0, local copies, waits for them, and re-layouts: 4.32 us -> none  [per_device(): picked = jnp.take(rows, where, axis=0)]
    dynamic_slice x0 -> x3, local copies, waits for them, and re-layouts: none -> 3.17 us  [per_device(): lax.dynamic_slice_in_dim(rows, where[r], 1, 0)]
    slice x1 -> x4, local copies, waits for them, and re-layouts: 0.08 us -> 2.22 us  [the longest x3 2.15 us: per_device(): where[r]]
  transfers between devices with their start and end apart: 3 -> 3, of which waited for: 3 -> 2; matrix products, arithmetic and copies ran while one was open for 3% -> 3% of each run, Pallas kernels for 0% -> 0%
where the time goes in v3:
time: 192 us; the launch traced here: 190 us
  between operations  104 us (54%)
  blocking collectives  27.5 us (14%)
  starting transfers between devices  21.6 us (11%)
  waiting for transfers between devices  18.5 us (10%)
  local copies, waits for them, and re-layouts  10.8 us (6%)
  matrix products  4.62 us (2%)
  other arithmetic  2.75 us (1%)
    all_gather x1, blocking collectives, per_device(): gathered = lax.all_gather(packed, 'dp', axis=0, tiled=True)  27.5 us
    all_to_all x1, starting transfers between devices, per_device(): lax.all_to_all(jnp.broadcast_to(assign[None], (ncent, pdev)), 'cent', 0,...  11.6 us
    all_to_all x1, starting transfers between devices, per_device(): lax.all_to_all(local_best.reshape(ncent, pdev), 'cent', 0, 0, tiled=True)  9.98 us
    all_to_all x1, waiting for transfers between devices, per_device(): lax.all_to_all(local_best.reshape(ncent, pdev), 'cent', 0, 0, tiled=True)  9.29 us
    all_to_all x1, waiting for transfers between devices, per_device(): lax.all_to_all(jnp.broadcast_to(assign[None], (ncent, pdev)), 'cent', 0,...  8.55 us
  transfers between devices with their start and end apart: 3, of which 2 were waited for; matrix products, arithmetic and copies ran while one was open for 3% of the time, Pallas kernels for 0%

profile of v3, /device:TPU:1, one launch (start us, length us, event | category | flops | bytes accessed | tf_op | source)
XLA Modules:
  0.0 189.9 jit_solution(10927698838485398030)
XLA Ops:
  7.2 0.0 copy-start.1
  7.2 0.0 all-gather.2.cloned.1.call-start
  7.2 0.7 all-gather.2.cloned.1.call-update
  7.9 1.3 broadcast_in_dim.22
  9.2 11.6 %all-to-all-start = ((s32[64,1,48]{2,1,0:T(1,128)}), s32[64,1,48]{2,1,0:T(1,128)S(1)}, u32[]{:S(2)}, u32[]{:S(2)}) async-start(s32[64,1,48]{2,1,0:T(1,128)} %broadcast_in_dim.22), calls=%async_computation | async-start | bytes 65536 | tf_op jit(solution)/shard_map/all_to_all | solution.py:19
  20.8 0.7 convert_element_type.53
  21.5 8.5 %all-to-all-done = s32[64,1,48]{2,1,0:T(1,128)S(1)} async-done(((s32[64,1,48]{2,1,0:T(1,128)}), s32[64,1,48]{2,1,0:T(1,128)S(1)}, u32[]{:S(2)}, u32[]{:S(2)}) %all-to-all-start) | async-done | bytes 12320 | tf_op jit(solution)/shard_map/all_to_all | solution.py:19
  30.1 0.2 subtract_reduce_fusion
  30.3 0.1 reshape.208
  30.3 0.3 reduce-window.9
  30.6 0.1 slice.215
  30.7 0.1 sub.29
  30.8 0.1 slice_reduce_fusion
  31.0 0.1 add_bitcast_fusion
  31.0 0.2 select_reduce_fusion
  31.3 0.7 fusion.8
  54.7 0.7 fusion.9
  80.3 0.7 fusion.10
  93.4 0.8 gather_fusion
  94.2 0.1 copy.13
  94.3 0.1 copy.14
  124.4 0.0 all-gather.2.cloned.1.call-done
  124.4 1.0 constant_dynamic-slice_fusion.36
  125.4 1.1 constant_dynamic-slice_fusion
  126.5 1.1 constant_dynamic-slice_fusion.18
  127.6 0.4 concatenate.6
  128.0 0.1 concatenate.7
  128.1 27.5 %all_gather.7 = bf16[384,1152]{1,0:T(8,128)(2,1)S(1)} all-gather(bf16[48,1152]{1,0:T(8,128)(2,1)S(1)} %concatenate.7), channel_id=1, replica_groups=mesh['dp'=8,'cent'=64] {'dp'}, dimensions={0}, use_global_device_ids=true | all-gather | bytes 995328 | tf_op jit(solution)/shard_map/all_gather | solution.py:37
  155.6 0.2 add_reduce_fusion
  155.8 0.0 copy-done.1
  155.8 0.0 copy-start.3
  155.8 0.9 multiply_reduce_fusion
  156.7 0.2 broadcast_multiply_fusion
  156.9 1.7 copy-done.3
  158.6 0.0 copy-start
  158.6 0.0 copy-start.2
  158.6 3.8 %convolution_reduce_fusion = f32[3072]{0:T(1024)S(1)} fusion(bf16[3072,1024]{1,0:T(8,128)(2,1)S(1)} %copy-done.3, f32[512,1024]{1,0:T(8,128)S(1)} %broadcast_multiply_fusion), kind=kOutput, calls=%fused_computation.3 | convolution fusion | flops 3223319552 | bytes 8400896 | tf_op jit(solution)/shard_map/dot_general | solution.py:45
  162.4 0.0 copy-done
  162.4 0.7 all_to_all.11
  163.1 10.0 %all-to-all-start.1 = ((f32[64,1,48]{2,1,0:T(1,128)}), f32[64,1,48]{2,1,0:T(1,128)S(1)}, u32[]{:S(2)}, u32[]{:S(2)}) async-start(f32[64,1,48]{2,1,0:T(1,128)} %bitcast.52), calls=%async_computation.1 | async-start | bytes 65536 | tf_op jit(solution)/shard_map/all_to_all | solution.py:47
  173.1 0.0 copy-done.2
  173.1 0.1 multiply_reduce_fusion.1
  173.2 9.3 %all-to-all-done.1 = f32[64,1,48]{2,1,0:T(1,128)S(1)} async-done(((f32[64,1,48]{2,1,0:T(1,128)}), f32[64,1,48]{2,1,0:T(1,128)S(1)}, u32[]{:S(2)}, u32[]{:S(2)}) %all-to-all-start.1) | async-done | bytes 12320 | tf_op jit(solution)/shard_map/all_to_all | solution.py:47
  182.5 0.1 reduce_max.19
  182.6 0.5 multiply_divide_fusion
  (7 shorter events, 0.1 us)
Async XLA Ops:
  7.2 148.6 %copy-start.1 = (f32[512,1024]{1,0:T(8,128)S(1)}, f32[512,1024]{1,0:T(8,128)}, u32[]{:S(2)}) copy-start(f32[512,1024]{1,0:T(8,128)} %param.6) | copy-start | bytes 6291460
  7.2 117.3 %all-gather.2.cloned.1.call-start = ((), (), s32[]{:S(2)}) async-start(), calls=%async_computation.2 | async-start | bytes 6389760 | tf_op jit(solution)/shard_map/all_gather | solution.py:18
  9.2 20.9 %all-to-all-start = ((s32[64,1,48]{2,1,0:T(1,128)}), s32[64,1,48]{2,1,0:T(1,128)S(1)}, u32[]{:S(2)}, u32[]{:S(2)}) async-start(s32[64,1,48]{2,1,0:T(1,128)} %broadcast_in_dim.22), calls=%async_computation | async-start | bytes 65536 | tf_op jit(solution)/shard_map/all_to_all | solution.py:19
  155.8 2.8 %copy-start.3 = (bf16[3072,1024]{1,0:T(8,128)(2,1)S(1)}, bf16[3072,1024]{1,0:T(8,128)(2,1)}, u32[]{:S(2)}) copy-start(bf16[3072,1024]{1,0:T(8,128)(2,1)} %all-gather.2.cloned.1.call-done) | copy-start | bytes 18874372
  158.6 3.8 %copy-start = (f32[512,1024]{1,0:T(8,128)}, f32[512,1024]{1,0:T(8,128)S(1)}, u32[]{:S(2)}) copy-start(f32[512,1024]{1,0:T(8,128)S(1)} %broadcast_multiply_fusion) | copy-start | bytes 6291460
  158.6 14.5 %copy-start.2 = (bf16[48,1024]{1,0:T(8,128)(2,1)S(1)}, bf16[48,1024]{1,0:T(8,128)(2,1)}, u32[]{:S(2)}) copy-start(bf16[48,1024]{1,0:T(8,128)(2,1)} %param.4) | copy-start | bytes 294916
  163.1 19.4 %all-to-all-start.1 = ((f32[64,1,48]{2,1,0:T(1,128)}), f32[64,1,48]{2,1,0:T(1,128)S(1)}, u32[]{:S(2)}, u32[]{:S(2)}) async-start(f32[64,1,48]{2,1,0:T(1,128)} %bitcast.52), calls=%async_computation.1 | async-start | bytes 65536 | tf_op jit(solution)/shard_map/all_to_all | solution.py:47
Sparse Core Ops, SparseCore 0:
  11.3 91.5 all-gather.1

commit v4 on v1

--- a/solution.py
+++ b/solution.py
@@ -24,8 +24,10 @@
         mine = (local >= 0) & (local < kdev)
         rank = jnp.cumsum(mine.astype(jnp.int32)) - 1
         pick = mine[None, :] & (rank[None, :] == jnp.arange(pdev, dtype=jnp.int32)[:, None])
-        picked = jnp.dot(pick.astype(jnp.bfloat16), rows, preferred_element_type=jnp.float32)
-        picked_label = jnp.sum(jnp.where(pick, local[None, :], 0), axis=1)
+        pick_rows, picked_label = lax.optimization_barrier(
+            (pick.astype(jnp.bfloat16), jnp.sum(jnp.where(pick, local[None, :], 0), axis=1))
+        )
+        picked = jnp.dot(pick_rows, rows, preferred_element_type=jnp.float32)
         hi = (picked_label // 16).astype(jnp.bfloat16)
         lo = (picked_label % 16).astype(jnp.bfloat16)
         packed = jnp.concatenate(

time: 167 us -> 167 us (level)
  no operation moved by 1% of the time
where the time goes in v4:
time: 167 us
  waiting for transfers between devices  89.8 us (54%)
  blocking collectives  23.1 us (14%)
  starting transfers between devices  22.7 us (14%)
  between operations  14.1 us (8%)
  matrix products  10.5 us (6%)
  local copies, waits for them, and re-layouts  3.94 us (2%)
  other arithmetic  2.83 us (2%)
    all_gather x1, waiting for transfers between devices, per_device(): rows = lax.all_gather(points, 'cent', axis=0, tiled=True)  71.3 us
    all_gather x1, blocking collectives, per_device(): gathered = lax.all_gather(packed, 'dp', axis=0, tiled=True)  23.1 us
    all_to_all x1, starting transfers between devices, per_device(): lax.all_to_all(jnp.broadcast_to(assign[None], (ncent, pdev)), 'cent', 0,...  11.6 us
    all_to_all x1, starting transfers between devices, per_device(): lax.all_to_all(local_best.reshape(ncent, pdev), 'cent', 0, 0, tiled=True)  11.1 us
    all_to_all x1, waiting for transfers between devices, per_device(): lax.all_to_all(local_best.reshape(ncent, pdev), 'cent', 0, 0, tiled=True)  9.18 us
    all_to_all x1, waiting for transfers between devices, per_device(): lax.all_to_all(jnp.broadcast_to(assign[None], (ncent, pdev)), 'cent', 0,...  8.55 us
    dot_general x1, matrix products, per_device(): picked = jnp.dot(pick_rows, rows, preferred_element_type=jnp.float32)  4.14 us
    dot_general x1, matrix products, per_device(): scores = jnp.dot(rows, rounded.T, preferred_element_type=jnp.float32)  3.75 us
  transfers between devices with their start and end apart: 3, of which 3 were waited for; matrix products, arithmetic and copies ran while one was open for 2% of the time, Pallas kernels for 0%

profile of v4, /device:TPU:1, one launch (start us, length us, event | category | flops | bytes accessed | tf_op | source)
XLA Modules:
  0.0 166.9 jit_solution(4449451637913037936)
XLA Ops:
  7.2 0.0 all-gather.2.cloned.1.call-start
  7.2 0.7 all-gather.2.cloned.1.call-update
  7.9 1.3 broadcast_in_dim.20
  9.2 11.6 %all-to-all-start = ((s32[64,1,48]{2,1,0:T(1,128)}), s32[64,1,48]{2,1,0:T(1,128)S(1)}, u32[]{:S(2)}, u32[]{:S(2)}) async-start(s32[64,1,48]{2,1,0:T(1,128)} %broadcast_in_dim.20), calls=%async_computation | async-start | bytes 65536 | tf_op jit(solution)/shard_map/all_to_all | solution.py:19
  20.8 0.7 convert_element_type.45
  21.5 8.5 %all-to-all-done = s32[64,1,48]{2,1,0:T(1,128)S(1)} async-done(((s32[64,1,48]{2,1,0:T(1,128)}), s32[64,1,48]{2,1,0:T(1,128)S(1)}, u32[]{:S(2)}, u32[]{:S(2)}) %all-to-all-start) | async-done | bytes 12320 | tf_op jit(solution)/shard_map/all_to_all | solution.py:19
  30.0 0.2 subtract_reduce_fusion
  30.2 0.1 reshape.95
  30.3 0.3 reduce-window.9
  30.6 0.1 slice.21
  30.7 0.1 sub.32
  30.8 0.1 slice_reduce_fusion
  30.9 0.1 add_bitcast_fusion
  31.0 0.2 select_reduce_fusion
  31.3 0.1 fusion.3
  31.4 0.1 copy.13
  31.5 0.1 copy.14
  31.6 71.3 %all-gather.2.cloned.1.call-done = bf16[3072,1024]{1,0:T(8,128)(2,1)} async-done(((bf16[48,1024]{1,0:T(8,128)(2,1)}), bf16[3072,1024]{1,0:T(8,128)(2,1)}) %all-gather.2.cloned.1.call-update) | async-done | bytes 6291472 | tf_op jit(solution)/shard_map/all_gather | solution.py:18
  102.9 0.0 slice-start
  102.9 4.1 %convolution_convert_fusion = bf16[48,1024]{1,0:T(8,128)(2,1)S(1)} fusion(bf16[48,3072]{1,0:T(8,128)(2,1)S(1)} %fusion.3, bf16[3072,1024]{1,0:T(8,128)(2,1)} %all-gather.2.cloned.1.call-done), kind=kOutput, calls=%fused_computation.3 | convolution fusion | flops 302039040 | bytes 6684672 | tf_op jit(solution)/shard_map/dot_general | solution.py:30
  107.1 0.1 concatenate.3
  107.2 23.1 %all_gather.7 = bf16[384,1152]{1,0:T(8,128)(2,1)S(1)} all-gather(bf16[48,1152]{1,0:T(8,128)(2,1)S(1)} %concatenate.3), channel_id=1, replica_groups=mesh['dp'=8,'cent'=64] {'dp'}, dimensions={0}, use_global_device_ids=true | all-gather | bytes 995328 | tf_op jit(solution)/shard_map/all_gather | solution.py:38
  130.3 0.2 add_reduce_fusion
  130.5 0.0 slice-start.1
  130.5 2.6 %multiply_reduce_fusion = (f32[512]{0:T(512)S(1)}, f32[512,1024]{1,0:T(8,128)S(1)}) fusion(bf16[384,1152]{1,0:T(8,128)(2,1)S(1)} %all_gather.7, s32[384]{0:T(512)S(1)} %add_reduce_fusion, f32[512,1024]{1,0:T(8,128)} %param.6, f32[512]{0:T(512)S(1)} %convert_element_type.45), kind=kOutput, calls=%fused_computation | convolution fusion | flops 404946432 | bytes 4986880 | tf_op jit(solution)/shard_map/dot_general | solution.py:42
  133.1 0.2 broadcast_multiply_fusion
  133.3 0.0 copy-start
  133.3 1.3 copy-done
  134.6 0.0 slice-done
  134.6 0.0 slice-done.1
  134.6 0.0 copy-start.1
  134.6 3.7 %convolution_reduce_fusion = f32[3072]{0:T(1024)S(1)} fusion(bf16[3072,1024]{1,0:T(8,128)(2,1)S(1)} %bitcast.11, f32[512,1024]{1,0:T(8,128)S(1)} %broadcast_multiply_fusion), kind=kOutput, calls=%fused_computation.2 | convolution fusion | flops 3223319552 | bytes 8400896 | tf_op jit(solution)/shard_map/dot_general | solution.py:46
  138.4 0.7 all_to_all.11
  139.1 11.1 %all-to-all-start.1 = ((f32[64,1,48]{2,1,0:T(1,128)}), f32[64,1,48]{2,1,0:T(1,128)S(1)}, u32[]{:S(2)}, u32[]{:S(2)}) async-start(f32[64,1,48]{2,1,0:T(1,128)} %bitcast.3), calls=%async_computation.1 | async-start | bytes 65536 | tf_op jit(solution)/shard_map/all_to_all | solution.py:48
  150.1 0.0 copy-done.1
  150.1 0.1 multiply_reduce_fusion.1
  150.3 9.2 %all-to-all-done.1 = f32[64,1,48]{2,1,0:T(1,128)S(1)} async-done(((f32[64,1,48]{2,1,0:T(1,128)}), f32[64,1,48]{2,1,0:T(1,128)S(1)}, u32[]{:S(2)}, u32[]{:S(2)}) %all-to-all-start.1) | async-done | bytes 12320 | tf_op jit(solution)/shard_map/all_to_all | solution.py:48
  159.4 0.1 reduce_max.19
  159.5 0.5 multiply_divide_fusion
  (6 shorter events, 0.1 us)
Async XLA Ops:
  7.2 95.8 %all-gather.2.cloned.1.call-start = ((), (), s32[]{:S(2)}) async-start(), calls=%async_computation.2 | async-start | bytes 6389760 | tf_op jit(solution)/shard_map/all_gather | solution.py:18
  9.2 20.9 %all-to-all-start = ((s32[64,1,48]{2,1,0:T(1,128)}), s32[64,1,48]{2,1,0:T(1,128)S(1)}, u32[]{:S(2)}, u32[]{:S(2)}) async-start(s32[64,1,48]{2,1,0:T(1,128)} %broadcast_in_dim.20), calls=%async_computation | async-start | bytes 65536 | tf_op jit(solution)/shard_map/all_to_all | solution.py:19
  102.9 31.7 %slice-start = ((s8[6291456]{0:T(1024)(128)(4,1)}), s8[2097152]{0:T(1024)(128)(4,1)S(1)}, s32[]{:S(2)}) async-start(s8[6291456]{0:T(1024)(128)(4,1)} %bitcast.10), calls=%async_computation.3 | async-start | bytes 4194304
  130.5 4.1 %slice-start.1 = ((s8[6291456]{0:T(1024)(128)(4,1)}), s8[4194304]{0:T(1024)(128)(4,1)S(1)}, s32[]{:S(2)}) async-start(s8[6291456]{0:T(1024)(128)(4,1)} %bitcast.10), calls=%async_computation.4 | async-start | bytes 8388608
  133.3 1.3 copy-start
  134.6 15.5 %copy-start.1 = (bf16[48,1024]{1,0:T(8,128)(2,1)S(1)}, bf16[48,1024]{1,0:T(8,128)(2,1)}, u32[]{:S(2)}) copy-start(bf16[48,1024]{1,0:T(8,128)(2,1)} %param.4) | copy-start | bytes 294916
  139.1 20.4 %all-to-all-start.1 = ((f32[64,1,48]{2,1,0:T(1,128)}), f32[64,1,48]{2,1,0:T(1,128)S(1)}, u32[]{:S(2)}, u32[]{:S(2)}) async-start(f32[64,1,48]{2,1,0:T(1,128)} %bitcast.3), calls=%async_computation.1 | async-start | bytes 65536 | tf_op jit(solution)/shard_map/all_to_all | solution.py:48
Sparse Core Ops, SparseCore 0:
  11.3 91.5 all-gather.1

commit v5 on v3

--- a/solution.py
+++ b/solution.py
@@ -1,7 +1,50 @@
 import jax
 import jax.numpy as jnp
 from jax import lax
+from jax.experimental import pallas as pl
+from jax.experimental.pallas import tpu as pltpu
 from jax.sharding import PartitionSpec as P
+
+SPAN = 8
+
+
+def _take_rows_kernel(where_ref, rows_hbm, out_ref, slabs, sems):
+    n = out_ref.shape[0]
+
+    def copy(r):
+        base = pl.multiple_of((where_ref[r] // SPAN) * SPAN, SPAN)
+        return pltpu.make_async_copy(rows_hbm.at[pl.ds(base, SPAN)], slabs.at[r], sems.at[r])
+
+    def start(r, carry):
+        copy(r).start()
+        return carry
+
+    def finish(r, carry):
+        copy(r).wait()
+        return carry
+
+    lax.fori_loop(0, n, start, 0)
+    lax.fori_loop(0, n, finish, 0)
+    offset = lax.broadcasted_iota(jnp.int32, (SPAN, out_ref.shape[1]), 0)
+    for r in range(n):
+        slab = slabs[r].astype(jnp.float32)
+        keep = offset == where_ref[r] % SPAN
+        out_ref[r : r + 1, :] = jnp.sum(jnp.where(keep, slab, 0.0), axis=0, keepdims=True)
+
+
+def take_rows(rows, where):
+    n, width = where.shape[0], rows.shape[1]
+    return pl.pallas_call(
+        _take_rows_kernel,
+        out_shape=jax.ShapeDtypeStruct((n, width), jnp.float32),
+        grid_spec=pltpu.PrefetchScalarGridSpec(
+            num_scalar_prefetch=1,
+            grid=(1,),
+            in_specs=[pl.BlockSpec(memory_space=pl.ANY)],
+            out_specs=pl.BlockSpec((n, width), lambda i, w: (0, 0)),
+            scratch_shapes=[pltpu.VMEM((n, SPAN, width), rows.dtype), pltpu.SemaphoreType.DMA((n,))],
+        ),
+    )(where, rows)
 
 
 def renorm(merged):
@@ -25,7 +68,7 @@
         rank = jnp.cumsum(mine.astype(jnp.int32)) - 1
         pick = mine[None, :] & (rank[None, :] == jnp.arange(pdev, dtype=jnp.int32)[:, None])
         where = jnp.sum(jnp.where(pick, jnp.arange(rows.shape[0], dtype=jnp.int32)[None, :], 0), axis=1)
-        picked = jnp.concatenate([lax.dynamic_slice_in_dim(rows, where[r], 1, 0) for r in range(pdev)], axis=0)
+        picked = take_rows(rows, where)
         picked_label = jnp.take(local, where, axis=0)
         hi = (picked_label // 16).astype(jnp.bfloat16)
         lo = (picked_label % 16).astype(jnp.bfloat16)

time: 192 us -> 168 us (0.88)
  between operations: 104 us -> 14.1 us
  waiting for transfers between devices: 18.5 us -> 89 us
  local copies, waits for them, and re-layouts: 10.8 us -> 4.7 us
  blocking collectives: 27.5 us -> 23.1 us
  Pallas kernels: 0 us -> 3.8 us
    all_gather x1, waiting for transfers between devices: 0.02 us -> 70.6 us  [per_device(): rows = lax.all_gather(points, 'cent', axis=0, tiled=True)]
    all_gather x1, blocking collectives: 27.5 us -> 23.1 us  [per_device(): gathered = lax.all_gather(packed, 'dp', axis=0, tiled=True)]
    pallas_call x0 -> x1, Pallas kernels: none -> 3.8 us  [take_rows(): pl.pallas_call(_take_rows_kernel, out_shape=jax.ShapeDtypeStruct((n, widt...]
    dynamic_slice x3 -> x0, local copies, waits for them, and re-layouts: 3.17 us -> none  [per_device(): lax.dynamic_slice_in_dim(rows, where[r], 1, 0)]
    slice x4 -> x1, local copies, waits for them, and re-layouts: 2.22 us -> 0.08 us  [the longest x3 2.15 us: per_device(): where[r]]
  transfers between devices with their start and end apart: 3 -> 3, of which waited for: 2 -> 3; matrix products, arithmetic and copies ran while one was open for 3% -> 3% of each run, Pallas kernels for 0% -> 0%
where the time goes in v5:
time: 168 us
  waiting for transfers between devices  89 us (53%)
  blocking collectives  23.1 us (14%)
  starting transfers between devices  22.7 us (14%)
  between operations  14.1 us (8%)
  matrix products  6.32 us (4%)
  local copies, waits for them, and re-layouts  4.7 us (3%)
  other arithmetic  3.82 us (2%)
  Pallas kernels  3.8 us (2%)
    all_gather x1, waiting for transfers between devices, per_device(): rows = lax.all_gather(points, 'cent', axis=0, tiled=True)  70.6 us
    all_gather x1, blocking collectives, per_device(): gathered = lax.all_gather(packed, 'dp', axis=0, tiled=True)  23.1 us
    all_to_all x1, starting transfers between devices, per_device(): lax.all_to_all(jnp.broadcast_to(assign[None], (ncent, pdev)), 'cent', 0,...  11.6 us
    all_to_all x1, starting transfers between devices, per_device(): lax.all_to_all(local_best.reshape(ncent, pdev), 'cent', 0, 0, tiled=True)  11.1 us
    all_to_all x1, waiting for transfers between devices, per_device(): lax.all_to_all(local_best.reshape(ncent, pdev), 'cent', 0, 0, tiled=True)  9.18 us
    all_to_all x1, waiting for transfers between devices, per_device(): lax.all_to_all(jnp.broadcast_to(assign[None], (ncent, pdev)), 'cent', 0,...  8.55 us
    pallas_call x1, Pallas kernels, take_rows(): pl.pallas_call(_take_rows_kernel, out_shape=jax.ShapeDtypeStruct((n, widt...  3.8 us
    dot_general x1, matrix products, per_device(): scores = jnp.dot(rows, rounded.T, preferred_element_type=jnp.float32)  3.75 us
  transfers between devices with their start and end apart: 3, of which 3 were waited for; matrix products, arithmetic and copies ran while one was open for 3% of the time, Pallas kernels for 0%

profile of v5, /device:TPU:1, one launch (start us, length us, event | category | flops | bytes accessed | tf_op | source)
XLA Modules:
  0.0 167.5 jit_solution(7296138513921234569)
XLA Ops:
  7.2 0.0 all-gather.2.cloned.1.call-start
  7.2 0.7 all-gather.2.cloned.1.call-update
  7.9 1.3 broadcast_in_dim.22
  9.2 11.6 %all-to-all-start = ((s32[64,1,48]{2,1,0:T(1,128)}), s32[64,1,48]{2,1,0:T(1,128)S(1)}, u32[]{:S(2)}, u32[]{:S(2)}) async-start(s32[64,1,48]{2,1,0:T(1,128)} %broadcast_in_dim.22), calls=%async_computation | async-start | bytes 65536 | tf_op jit(solution)/shard_map/all_to_all | solution.py:62
  20.8 0.7 convert_element_type.56
  21.5 8.5 %all-to-all-done = s32[64,1,48]{2,1,0:T(1,128)S(1)} async-done(((s32[64,1,48]{2,1,0:T(1,128)}), s32[64,1,48]{2,1,0:T(1,128)S(1)}, u32[]{:S(2)}, u32[]{:S(2)}) %all-to-all-start) | async-done | bytes 12320 | tf_op jit(solution)/shard_map/all_to_all | solution.py:62
  30.0 0.2 subtract_reduce_fusion
  30.2 0.1 reshape.208
  30.3 0.3 reduce-window.9
  30.6 0.1 slice.23
  30.7 0.1 sub.29
  30.8 0.1 slice_reduce_fusion
  30.9 0.1 add_bitcast_fusion
  31.0 0.2 select_reduce_fusion.where_ref
  31.3 0.0 copy-start.2
  31.3 0.1 copy.19
  31.4 0.1 fusion.8
  31.5 0.8 gather_fusion
  32.3 0.1 copy.22
  32.4 70.6 %all-gather.2.cloned.1.call-done.rows_hbm = bf16[3072,1024]{1,0:T(8,128)(2,1)} async-done(((bf16[48,1024]{1,0:T(8,128)(2,1)}), bf16[3072,1024]{1,0:T(8,128)(2,1)}) %all-gather.2.cloned.1.call-update) | async-done | bytes 6291472 | tf_op jit(solution)/shard_map/all_gather | solution.py:61
  102.9 0.0 copy-done.2
  102.9 0.0 slice-start
  102.9 3.8 %shard_map.59 = f32[48,1024]{1,0:T(8,128)} custom-call(s32[48]{0:T(128)} %copy-done.2, bf16[3072,1024]{1,0:T(8,128)(2,1)} %all-gather.2.cloned.1.call-done.rows_hbm), custom_call_target="tpu_custom_call" | custom-call | tf_op jit(solution)/shard_map/pallas_call | solution.py:37
  106.8 0.9 convert_element_type.59
  107.7 0.1 concatenate.3
  107.8 23.1 %all_gather.7 = bf16[384,1152]{1,0:T(8,128)(2,1)S(1)} all-gather(bf16[48,1152]{1,0:T(8,128)(2,1)S(1)} %concatenate.3), channel_id=1, replica_groups=mesh['dp'=8,'cent'=64] {'dp'}, dimensions={0}, use_global_device_ids=true | all-gather | bytes 995328 | tf_op jit(solution)/shard_map/all_gather | solution.py:80
  130.9 0.2 add_reduce_fusion
  131.1 0.0 slice-start.1
  131.1 2.6 %multiply_reduce_fusion = (f32[512]{0:T(512)S(1)}, f32[512,1024]{1,0:T(8,128)S(1)}) fusion(bf16[384,1152]{1,0:T(8,128)(2,1)S(1)} %all_gather.7, s32[384]{0:T(512)S(1)} %add_reduce_fusion, f32[512,1024]{1,0:T(8,128)} %param.6, f32[512]{0:T(512)S(1)} %convert_element_type.56), kind=kOutput, calls=%fused_computation.1 | convolution fusion | flops 404946432 | bytes 4986880 | tf_op jit(solution)/shard_map/dot_general | solution.py:84
  133.7 0.2 broadcast_multiply_fusion
  133.9 0.0 copy-start
  133.9 1.3 copy-done
  135.2 0.0 slice-done
  135.2 0.0 slice-done.1
  135.2 0.0 copy-start.1
  135.2 3.8 %convolution_reduce_fusion = f32[3072]{0:T(1024)S(1)} fusion(bf16[3072,1024]{1,0:T(8,128)(2,1)S(1)} %bitcast.7, f32[512,1024]{1,0:T(8,128)S(1)} %broadcast_multiply_fusion), kind=kOutput, calls=%fused_computation.3 | convolution fusion | flops 3223319552 | bytes 8400896 | tf_op jit(solution)/shard_map/dot_general | solution.py:88
  139.0 0.7 all_to_all.11
  139.7 11.1 %all-to-all-start.1 = ((f32[64,1,48]{2,1,0:T(1,128)}), f32[64,1,48]{2,1,0:T(1,128)S(1)}, u32[]{:S(2)}, u32[]{:S(2)}) async-start(f32[64,1,48]{2,1,0:T(1,128)} %bitcast.3), calls=%async_computation.1 | async-start | bytes 65536 | tf_op jit(solution)/shard_map/all_to_all | solution.py:90
  150.7 0.0 copy-done.1
  150.8 0.1 multiply_reduce_fusion.1
  150.9 9.2 %all-to-all-done.1 = f32[64,1,48]{2,1,0:T(1,128)S(1)} async-done(((f32[64,1,48]{2,1,0:T(1,128)}), f32[64,1,48]{2,1,0:T(1,128)S(1)}, u32[]{:S(2)}, u32[]{:S(2)}) %all-to-all-start.1) | async-done | bytes 12320 | tf_op jit(solution)/shard_map/all_to_all | solution.py:90
  160.1 0.1 reduce_max.19
  160.1 0.5 multiply_divide_fusion
  (7 shorter events, 0.1 us)
Async XLA Ops:
  7.2 95.8 %all-gather.2.cloned.1.call-start = ((), (), s32[]{:S(2)}) async-start(), calls=%async_computation.2 | async-start | bytes 6389760 | tf_op jit(solution)/shard_map/all_gather | solution.py:61
  9.2 20.9 %all-to-all-start = ((s32[64,1,48]{2,1,0:T(1,128)}), s32[64,1,48]{2,1,0:T(1,128)S(1)}, u32[]{:S(2)}, u32[]{:S(2)}) async-start(s32[64,1,48]{2,1,0:T(1,128)} %broadcast_in_dim.22), calls=%async_computation | async-start | bytes 65536 | tf_op jit(solution)/shard_map/all_to_all | solution.py:62
  31.3 71.7 %copy-start.2 = (s32[48]{0:T(128)}, s32[48]{0:T(128)S(1)}, u32[]{:S(2)}) copy-start(s32[48]{0:T(128)S(1)} %select_reduce_fusion.where_ref) | copy-start | bytes 580
  102.9 32.3 %slice-start = ((s8[6291456]{0:T(1024)(128)(4,1)}), s8[2097152]{0:T(1024)(128)(4,1)S(1)}, s32[]{:S(2)}) async-start(s8[6291456]{0:T(1024)(128)(4,1)} %bitcast.6), calls=%async_computation.3 | async-start | bytes 4194304
  131.1 4.1 %slice-start.1 = ((s8[6291456]{0:T(1024)(128)(4,1)}), s8[4194304]{0:T(1024)(128)(4,1)S(1)}, s32[]{:S(2)}) async-start(s8[6291456]{0:T(1024)(128)(4,1)} %bitcast.6), calls=%async_computation.4 | async-start | bytes 8388608
  133.9 1.3 copy-start
  135.2 15.5 %copy-start.1 = (bf16[48,1024]{1,0:T(8,128)(2,1)S(1)}, bf16[48,1024]{1,0:T(8,128)(2,1)}, u32[]{:S(2)}) copy-start(bf16[48,1024]{1,0:T(8,128)(2,1)} %param.4) | copy-start | bytes 294916
  139.7 20.4 %all-to-all-start.1 = ((f32[64,1,48]{2,1,0:T(1,128)}), f32[64,1,48]{2,1,0:T(1,128)S(1)}, u32[]{:S(2)}, u32[]{:S(2)}) async-start(f32[64,1,48]{2,1,0:T(1,128)} %bitcast.3), calls=%async_computation.1 | async-start | bytes 65536 | tf_op jit(solution)/shard_map/all_to_all | solution.py:90
Sparse Core Ops, SparseCore 0:
  11.3 91.5 all-gather.1

commit v6 on v2

--- a/solution.py
+++ b/solution.py
@@ -1,7 +1,33 @@
 import jax
 import jax.numpy as jnp
 from jax import lax
+from jax.experimental import pallas as pl
+from jax.experimental.pallas import tpu as pltpu
 from jax.sharding import PartitionSpec as P
+
+BLOCK = 512
+
+
+def _best_kernel(cent_ref, rows_ref, out_ref):
+    scores = lax.dot_general(
+        cent_ref[...], rows_ref[...], (((1,), (1,)), ((), ())), preferred_element_type=jnp.float32
+    )
+    out_ref[...] = jnp.max(scores, axis=0, keepdims=True)
+
+
+def best_scores(rows, rounded):
+    n, width = rows.shape
+    k = rounded.shape[0]
+    return pl.pallas_call(
+        _best_kernel,
+        out_shape=jax.ShapeDtypeStruct((1, n), jnp.float32),
+        grid=(n // BLOCK,),
+        in_specs=[
+            pl.BlockSpec((k, width), lambda i: (0, 0)),
+            pl.BlockSpec((BLOCK, width), lambda i: (i, 0)),
+        ],
+        out_specs=pl.BlockSpec((1, BLOCK), lambda i: (0, i)),
+    )(rounded, rows).reshape(n)
 
 
 def renorm(merged):
@@ -42,8 +68,7 @@
 
         fresh = renorm(weighted + total)
         rounded = fresh.astype(jnp.bfloat16)
-        scores = jnp.dot(rows, rounded.T, preferred_element_type=jnp.float32)
-        local_best = jnp.max(scores, axis=1)
+        local_best = best_scores(rows, rounded)
         top = jnp.max(lax.all_to_all(local_best.reshape(ncent, pdev), "cent", 0, 0, tiled=True), axis=0)
         values = points.astype(jnp.float32)
         scale = width * jnp.sqrt(jnp.mean(values * values, axis=1) + 1e-06)

time: 166 us -> 172 us (1.036)
  Pallas kernels: 0 us -> 7.83 us
  matrix products: 4.62 us -> 0.85 us
  other arithmetic: 2.96 us -> 6.11 us
    pallas_call x0 -> x1, Pallas kernels: none -> 7.83 us  [best_scores(): pl.pallas_call(_best_kernel, out_shape=jax.ShapeDtypeStruct((1, n), jnp.f...]
    dot_general x1 -> x0, matrix products: 3.76 us -> none  [per_device(): scores = jnp.dot(rows, rounded.T, preferred_element_type=jnp.float32)]
    convert_element_type x0 -> x1, other arithmetic: none -> 1.98 us  [per_device(): rounded = fresh.astype(jnp.bfloat16)]
where the time goes in v6:
time: 172 us
  waiting for transfers between devices  88.9 us (52%)
  blocking collectives  23.1 us (13%)
  starting transfers between devices  22.7 us (13%)
  between operations  14.1 us (8%)
  local copies, waits for them, and re-layouts  8.22 us (5%)
  Pallas kernels  7.83 us (5%)
  other arithmetic  6.11 us (4%)
    all_gather x1, waiting for transfers between devices, per_device(): rows = lax.all_gather(points, 'cent', axis=0, tiled=True)  70.5 us
    all_gather x1, blocking collectives, per_device(): gathered = lax.all_gather(packed, 'dp', axis=0, tiled=True)  23.1 us
    all_to_all x1, starting transfers between devices, per_device(): lax.all_to_all(jnp.broadcast_to(assign[None], (ncent, pdev)), 'cent', 0,...  11.6 us
    all_to_all x1, starting transfers between devices, per_device(): lax.all_to_all(local_best.reshape(ncent, pdev), 'cent', 0, 0, tiled=True)  11.1 us
    all_to_all x1, waiting for transfers between devices, per_device(): lax.all_to_all(local_best.reshape(ncent, pdev), 'cent', 0, 0, tiled=True)  9.18 us
    all_to_all x1, waiting for transfers between devices, per_device(): lax.all_to_all(jnp.broadcast_to(assign[None], (ncent, pdev)), 'cent', 0,...  8.55 us
    pallas_call x1, Pallas kernels, best_scores(): pl.pallas_call(_best_kernel, out_shape=jax.ShapeDtypeStruct((1, n), jnp.f...  7.83 us
    gather x1, local copies, waits for them, and re-layouts, per_device(): picked = jnp.take(rows, where, axis=0)  4.32 us
  transfers between devices with their start and end apart: 3, of which 3 were waited for; matrix products, arithmetic and copies ran while one was open for 3% of the time, Pallas kernels for 0%

profile of v6, /device:TPU:1, one launch (start us, length us, event | category | flops | bytes accessed | tf_op | source)
XLA Modules:
  0.0 171.9 jit_solution(11638867318542778491)
XLA Ops:
  7.2 0.0 copy-start
  7.2 0.0 all-gather.2.cloned.1.call-start
  7.2 0.7 all-gather.2.cloned.1.call-update
  7.9 1.3 broadcast_in_dim.32
  9.2 11.6 %all-to-all-start = ((s32[64,1,48]{2,1,0:T(1,128)}), s32[64,1,48]{2,1,0:T(1,128)S(1)}, u32[]{:S(2)}, u32[]{:S(2)}) async-start(s32[64,1,48]{2,1,0:T(1,128)} %broadcast_in_dim.32), calls=%async_computation | async-start | bytes 65536 | tf_op jit(solution)/shard_map/all_to_all | solution.py:45
  20.8 0.7 convert_element_type.53
  21.5 8.5 %all-to-all-done = s32[64,1,48]{2,1,0:T(1,128)S(1)} async-done(((s32[64,1,48]{2,1,0:T(1,128)}), s32[64,1,48]{2,1,0:T(1,128)S(1)}, u32[]{:S(2)}, u32[]{:S(2)}) %all-to-all-start) | async-done | bytes 12320 | tf_op jit(solution)/shard_map/all_to_all | solution.py:45
  30.1 0.2 subtract_reduce_fusion
  30.3 0.1 reshape.207
  30.3 0.3 reduce-window.9
  30.6 0.1 slice.25
  30.7 0.1 sub.29
  30.8 0.1 slice_reduce_fusion
  31.0 0.1 add_bitcast_fusion
  31.0 0.2 select_reduce_fusion
  31.3 0.1 copy.19
  31.4 0.1 fusion.7
  31.5 0.8 gather_fusion.1
  32.3 0.1 copy.22
  32.4 70.5 %all-gather.2.cloned.1.call-done.rows_ref = bf16[3072,1024]{1,0:T(8,128)(2,1)} async-done(((bf16[48,1024]{1,0:T(8,128)(2,1)}), bf16[3072,1024]{1,0:T(8,128)(2,1)}) %all-gather.2.cloned.1.call-update) | async-done | bytes 6291472 | tf_op jit(solution)/shard_map/all_gather | solution.py:44
  103.0 4.3 %gather_fusion = bf16[48,1024]{1,0:T(8,128)(2,1)S(1)} fusion(bf16[3072,1024]{1,0:T(8,128)(2,1)} %all-gather.2.cloned.1.call-done.rows_ref, s32[1024]{0:T(1024)S(1)} %pad_clamp_fusion), kind=kCustom, calls=%fused_computation | custom fusion | bytes 196800 | tf_op jit(solution)/shard_map/jit(_take)/gather | solution.py:54
  107.3 0.1 broadcast_select_fusion
  107.4 0.1 concatenate.3
  107.5 23.1 %all_gather.7 = bf16[384,1152]{1,0:T(8,128)(2,1)S(1)} all-gather(bf16[48,1152]{1,0:T(8,128)(2,1)S(1)} %concatenate.3), channel_id=1, replica_groups=mesh['dp'=8,'cent'=64] {'dp'}, dimensions={0}, use_global_device_ids=true | all-gather | bytes 995328 | tf_op jit(solution)/shard_map/all_gather | solution.py:63
  130.5 0.2 add_reduce_fusion
  130.8 0.0 copy-done
  130.8 0.9 multiply_reduce_fusion
  131.6 2.0 %fusion.9 = (bf16[512,1024]{1,0:T(8,128)(2,1)}, f32[512,1024]{1,0:T(8,128)}) fusion(f32[512,1024]{1,0:T(8,128)S(1)} %get-tuple-element.9, f32[512]{0:T(512)S(1)} %add_rsqrt_fusion), kind=kLoop, calls=%fused_computation.38 | loop fusion | flops 1048576 | bytes 5244928 | tf_op jit(solution)/shard_map/convert_element_type | solution.py:70
  133.6 0.0 copy-start.1
  133.6 7.8 %shard_map.59 = f32[1,3072]{1,0:T(1,128)} custom-call(bf16[512,1024]{1,0:T(8,128)(2,1)} %get-tuple-element.4.cent_ref, bf16[3072,1024]{1,0:T(8,128)(2,1)} %all-gather.2.cloned.1.call-done.rows_ref), custom_call_target="tpu_custom_call" | custom-call | tf_op jit(solution)/shard_map/pallas_call | solution.py:21
  141.4 0.5 broadcast.246
  142.0 1.4 reduce.18
  143.3 0.7 all_to_all.11
  144.0 11.1 %all-to-all-start.1 = ((f32[64,1,48]{2,1,0:T(1,128)}), f32[64,1,48]{2,1,0:T(1,128)S(1)}, u32[]{:S(2)}, u32[]{:S(2)}) async-start(f32[64,1,48]{2,1,0:T(1,128)} %bitcast.3), calls=%async_computation.1 | async-start | bytes 65536 | tf_op jit(solution)/shard_map/all_to_all | solution.py:72
  155.1 0.0 copy-done.1
  155.1 0.1 multiply_reduce_fusion.1
  155.2 9.2 %all-to-all-done.1 = f32[64,1,48]{2,1,0:T(1,128)S(1)} async-done(((f32[64,1,48]{2,1,0:T(1,128)}), f32[64,1,48]{2,1,0:T(1,128)S(1)}, u32[]{:S(2)}, u32[]{:S(2)}) %all-to-all-start.1) | async-done | bytes 12320 | tf_op jit(solution)/shard_map/all_to_all | solution.py:72
  164.4 0.1 reduce_max.9
  164.5 0.5 multiply_divide_fusion
  (7 shorter events, 0.1 us)
Async XLA Ops:
  7.2 123.6 %copy-start = (f32[512,1024]{1,0:T(8,128)S(1)}, f32[512,1024]{1,0:T(8,128)}, u32[]{:S(2)}) copy-start(f32[512,1024]{1,0:T(8,128)} %param.6) | copy-start | bytes 6291460
  7.2 95.8 %all-gather.2.cloned.1.call-start = ((), (), s32[]{:S(2)}) async-start(), calls=%async_computation.2 | async-start | bytes 6389760 | tf_op jit(solution)/shard_map/all_gather | solution.py:44
  9.2 20.9 %all-to-all-start = ((s32[64,1,48]{2,1,0:T(1,128)}), s32[64,1,48]{2,1,0:T(1,128)S(1)}, u32[]{:S(2)}, u32[]{:S(2)}) async-start(s32[64,1,48]{2,1,0:T(1,128)} %broadcast_in_dim.32), calls=%async_computation | async-start | bytes 65536 | tf_op jit(solution)/shard_map/all_to_all | solution.py:45
  133.6 21.5 %copy-start.1 = (bf16[48,1024]{1,0:T(8,128)(2,1)S(1)}, bf16[48,1024]{1,0:T(8,128)(2,1)}, u32[]{:S(2)}) copy-start(bf16[48,1024]{1,0:T(8,128)(2,1)} %param.4) | copy-start | bytes 294916
  144.0 20.4 %all-to-all-start.1 = ((f32[64,1,48]{2,1,0:T(1,128)}), f32[64,1,48]{2,1,0:T(1,128)S(1)}, u32[]{:S(2)}, u32[]{:S(2)}) async-start(f32[64,1,48]{2,1,0:T(1,128)} %bitcast.3), calls=%async_computation.1 | async-start | bytes 65536 | tf_op jit(solution)/shard_map/all_to_all | solution.py:72
Sparse Core Ops, SparseCore 0:
  11.3 91.5 all-gather.1

commit v7 on v2

--- a/solution.py
+++ b/solution.py
@@ -43,11 +43,11 @@
         fresh = renorm(weighted + total)
         rounded = fresh.astype(jnp.bfloat16)
         scores = jnp.dot(rows, rounded.T, preferred_element_type=jnp.float32)
-        local_best = jnp.max(scores, axis=1)
-        top = jnp.max(lax.all_to_all(local_best.reshape(ncent, pdev), "cent", 0, 0, tiled=True), axis=0)
+        local_best = jnp.max(scores.reshape(ncent, pdev, kdev), axis=2)
+        received = lax.all_to_all(local_best, "cent", 0, 0, tiled=True)
         values = points.astype(jnp.float32)
         scale = width * jnp.sqrt(jnp.mean(values * values, axis=1) + 1e-06)
-        return (fresh, top / scale)
+        return (fresh, jnp.max(received / scale[None, :], axis=0))
 
     return per_device
 

time: 166 us -> 166 us (level)
  no operation moved by 1% of the time
where the time goes in v7:
time: 166 us
  waiting for transfers between devices  88.1 us (53%)
  blocking collectives  23.1 us (14%)
  starting transfers between devices  22.7 us (14%)
  between operations  14.2 us (9%)
  local copies, waits for them, and re-layouts  9.42 us (6%)
  matrix products  4.59 us (3%)
  other arithmetic  3.79 us (2%)
    all_gather x1, waiting for transfers between devices, per_device(): rows = lax.all_gather(points, 'cent', axis=0, tiled=True)  70.5 us
    all_gather x1, blocking collectives, per_device(): gathered = lax.all_gather(packed, 'dp', axis=0, tiled=True)  23.1 us
    all_to_all x1, starting transfers between devices, per_device(): lax.all_to_all(jnp.broadcast_to(assign[None], (ncent, pdev)), 'cent', 0,...  11.6 us
    all_to_all x1, starting transfers between devices, per_device(): received = lax.all_to_all(local_best, 'cent', 0, 0, tiled=True)  11.1 us
    all_to_all x1, waiting for transfers between devices, per_device(): received = lax.all_to_all(local_best, 'cent', 0, 0, tiled=True)  9.3 us
    all_to_all x1, waiting for transfers between devices, per_device(): lax.all_to_all(jnp.broadcast_to(assign[None], (ncent, pdev)), 'cent', 0,...  7.53 us
    gather x1, local copies, waits for them, and re-layouts, per_device(): picked = jnp.take(rows, where, axis=0)  4.32 us
    dot_general x1, matrix products, per_device(): scores = jnp.dot(rows, rounded.T, preferred_element_type=jnp.float32)  3.76 us
  transfers between devices with their start and end apart: 3, of which 3 were waited for; matrix products, arithmetic and copies ran while one was open for 3% of the time, Pallas kernels for 0%

profile of v7, /device:TPU:1, one launch (start us, length us, event | category | flops | bytes accessed | tf_op | source)
XLA Modules:
  0.0 165.8 jit_solution(1306409276618937855)
XLA Ops:
  7.2 0.0 copy-start.1
  7.2 0.0 all-gather.2.cloned.1.call-start
  7.2 0.7 all-gather.2.cloned.1.call-update
  7.9 1.3 broadcast_in_dim.32
  9.2 11.6 %all-to-all-start = ((s32[64,1,48]{2,1,0:T(1,128)}), s32[64,1,48]{2,1,0:T(1,128)S(1)}, u32[]{:S(2)}, u32[]{:S(2)}) async-start(s32[64,1,48]{2,1,0:T(1,128)} %broadcast_in_dim.32), calls=%async_computation | async-start | bytes 65536 | tf_op jit(solution)/shard_map/all_to_all | solution.py:19
  20.8 1.0 multiply_reduce_fusion.1
  21.8 0.7 convert_element_type.53
  22.5 7.5 %all-to-all-done = s32[64,1,48]{2,1,0:T(1,128)S(1)} async-done(((s32[64,1,48]{2,1,0:T(1,128)}), s32[64,1,48]{2,1,0:T(1,128)S(1)}, u32[]{:S(2)}, u32[]{:S(2)}) %all-to-all-start) | async-done | bytes 12320 | tf_op jit(solution)/shard_map/all_to_all | solution.py:19
  30.1 0.2 subtract_reduce_fusion
  30.3 0.1 reshape.215
  30.3 0.3 reduce-window.9
  30.6 0.1 slice.25
  30.7 0.1 sub.29
  30.8 0.1 slice_reduce_fusion
  30.9 0.1 add_bitcast_fusion
  31.0 0.2 select_reduce_fusion
  31.3 0.1 copy.19
  31.4 0.1 fusion.8
  31.5 0.8 gather_fusion.1
  32.3 0.1 copy.22
  32.4 70.5 %all-gather.2.cloned.1.call-done = bf16[3072,1024]{1,0:T(8,128)(2,1)} async-done(((bf16[48,1024]{1,0:T(8,128)(2,1)}), bf16[3072,1024]{1,0:T(8,128)(2,1)}) %all-gather.2.cloned.1.call-update) | async-done | bytes 6291472 | tf_op jit(solution)/shard_map/all_gather | solution.py:18
  103.0 4.3 %gather_fusion = bf16[48,1024]{1,0:T(8,128)(2,1)S(1)} fusion(bf16[3072,1024]{1,0:T(8,128)(2,1)} %all-gather.2.cloned.1.call-done, s32[1024]{0:T(1024)S(1)} %pad_clamp_fusion), kind=kCustom, calls=%fused_computation | custom fusion | bytes 196800 | tf_op jit(solution)/shard_map/jit(_take)/gather | solution.py:28
  107.3 0.1 broadcast_select_fusion
  107.4 0.1 concatenate.3
  107.5 23.1 %all_gather.7 = bf16[384,1152]{1,0:T(8,128)(2,1)S(1)} all-gather(bf16[48,1152]{1,0:T(8,128)(2,1)S(1)} %concatenate.3), channel_id=1, replica_groups=mesh['dp'=8,'cent'=64] {'dp'}, dimensions={0}, use_global_device_ids=true | all-gather | bytes 995328 | tf_op jit(solution)/shard_map/all_gather | solution.py:37
  130.5 0.2 add_reduce_fusion
  130.8 0.0 copy-done.1
  130.8 0.0 copy-start.2
  130.8 0.8 multiply_reduce_fusion
  131.6 0.2 broadcast_multiply_fusion
  131.8 1.7 %copy-done.2 = bf16[3072,1024]{1,0:T(8,128)(2,1)S(1)} copy-done((bf16[3072,1024]{1,0:T(8,128)(2,1)S(1)}, bf16[3072,1024]{1,0:T(8,128)(2,1)}, u32[]{:S(2)}) %copy-start.2) | copy-done | bytes 6291480
  133.6 0.0 copy-start
  133.6 3.8 %convolution_reduce_fusion = f32[3072]{0:T(1024)S(1)} fusion(bf16[3072,1024]{1,0:T(8,128)(2,1)S(1)} %copy-done.2, f32[512,1024]{1,0:T(8,128)S(1)} %broadcast_multiply_fusion), kind=kOutput, calls=%fused_computation.4 | convolution fusion | flops 3223319552 | bytes 8400896 | tf_op jit(solution)/shard_map/dot_general | solution.py:45
  137.3 0.0 copy-done
  137.3 0.7 all_to_all.13
  138.0 11.1 %all-to-all-start.1 = ((f32[64,1,48]{2,1,0:T(1,128)}), f32[64,1,48]{2,1,0:T(1,128)S(1)}, u32[]{:S(2)}, u32[]{:S(2)}) async-start(f32[64,1,48]{2,1,0:T(1,128)} %bitcast.3), calls=%async_computation.1 | async-start | bytes 65536 | tf_op jit(solution)/shard_map/all_to_all | solution.py:47
  149.1 9.3 %all-to-all-done.1 = f32[64,1,48]{2,1,0:T(1,128)S(1)} async-done(((f32[64,1,48]{2,1,0:T(1,128)}), f32[64,1,48]{2,1,0:T(1,128)S(1)}, u32[]{:S(2)}, u32[]{:S(2)}) %all-to-all-start.1) | async-done | bytes 12320 | tf_op jit(solution)/shard_map/all_to_all | solution.py:47
  158.4 0.5 divide_reduce_fusion
  (8 shorter events, 0.1 us)
Async XLA Ops:
  7.2 123.6 %copy-start.1 = (f32[512,1024]{1,0:T(8,128)S(1)}, f32[512,1024]{1,0:T(8,128)}, u32[]{:S(2)}) copy-start(f32[512,1024]{1,0:T(8,128)} %param.6) | copy-start | bytes 6291460
  7.2 95.8 %all-gather.2.cloned.1.call-start = ((), (), s32[]{:S(2)}) async-start(), calls=%async_computation.2 | async-start | bytes 6389760 | tf_op jit(solution)/shard_map/all_gather | solution.py:18
  9.2 20.9 %all-to-all-start = ((s32[64,1,48]{2,1,0:T(1,128)}), s32[64,1,48]{2,1,0:T(1,128)S(1)}, u32[]{:S(2)}, u32[]{:S(2)}) async-start(s32[64,1,48]{2,1,0:T(1,128)} %broadcast_in_dim.32), calls=%async_computation | async-start | bytes 65536 | tf_op jit(solution)/shard_map/all_to_all | solution.py:19
  130.8 2.8 %copy-start.2 = (bf16[3072,1024]{1,0:T(8,128)(2,1)S(1)}, bf16[3072,1024]{1,0:T(8,128)(2,1)}, u32[]{:S(2)}) copy-start(bf16[3072,1024]{1,0:T(8,128)(2,1)} %all-gather.2.cloned.1.call-done) | copy-start | bytes 18874372
  133.6 3.8 %copy-start = (f32[512,1024]{1,0:T(8,128)}, f32[512,1024]{1,0:T(8,128)S(1)}, u32[]{:S(2)}) copy-start(f32[512,1024]{1,0:T(8,128)S(1)} %broadcast_multiply_fusion) | copy-start | bytes 6291460
  138.0 20.4 %all-to-all-start.1 = ((f32[64,1,48]{2,1,0:T(1,128)}), f32[64,1,48]{2,1,0:T(1,128)S(1)}, u32[]{:S(2)}, u32[]{:S(2)}) async-start(f32[64,1,48]{2,1,0:T(1,128)} %bitcast.3), calls=%async_computation.1 | async-start | bytes 65536 | tf_op jit(solution)/shard_map/all_to_all | solution.py:47
Sparse Core Ops, SparseCore 0:
  11.3 91.5 all-gather.1

commit v8 on v7

--- a/solution.py
+++ b/solution.py
@@ -1,7 +1,31 @@
 import jax
 import jax.numpy as jnp
 from jax import lax
+from jax.experimental import pallas as pl
+from jax.experimental.pallas import tpu as pltpu
 from jax.sharding import PartitionSpec as P
+
+BLOCK = 1024
+
+
+def _best_kernel(rows_ref, cent_t_ref, out_ref):
+    scores = jnp.dot(rows_ref[...], cent_t_ref[...], preferred_element_type=jnp.float32)
+    out_ref[...] = jnp.max(scores, axis=1, keepdims=True)
+
+
+def best_scores(rows, cent_t):
+    n, width = rows.shape
+    k = cent_t.shape[1]
+    return pl.pallas_call(
+        _best_kernel,
+        out_shape=jax.ShapeDtypeStruct((n, 1), jnp.float32),
+        grid=(n // BLOCK,),
+        in_specs=[
+            pl.BlockSpec((BLOCK, width), lambda i: (i, 0)),
+            pl.BlockSpec((width, k), lambda i: (0, 0)),
+        ],
+        out_specs=pl.BlockSpec((BLOCK, 1), lambda i: (i, 0)),
+    )(rows, cent_t)
 
 
 def renorm(merged):
@@ -42,8 +66,7 @@
 
         fresh = renorm(weighted + total)
         rounded = fresh.astype(jnp.bfloat16)
-        scores = jnp.dot(rows, rounded.T, preferred_element_type=jnp.float32)
-        local_best = jnp.max(scores.reshape(ncent, pdev, kdev), axis=2)
+        local_best = best_scores(rows, rounded.T).reshape(ncent, pdev)
         received = lax.all_to_all(local_best, "cent", 0, 0, tiled=True)
         values = points.astype(jnp.float32)
         scale = width * jnp.sqrt(jnp.mean(values * values, axis=1) + 1e-06)

time: 166 us -> 171 us (1.030)
  Pallas kernels: 0 us -> 7.08 us
  matrix products: 4.59 us -> 0.84 us
  waiting for transfers between devices: 88.1 us -> 85 us
  other arithmetic: 3.79 us -> 6.11 us
  local copies, waits for them, and re-layouts: 9.42 us -> 11.5 us
    pallas_call x0 -> x1, Pallas kernels: none -> 7.08 us  [best_scores(): pl.pallas_call(_best_kernel, out_shape=jax.ShapeDtypeStruct((n, 1), jnp.f...]
    dot_general x1 -> x0, matrix products: 3.76 us -> none  [per_device(): scores = jnp.dot(rows, rounded.T, preferred_element_type=jnp.float32)]
    unnamed x6 -> x4, local copies, waits for them, and re-layouts: 1.73 us -> 3.75 us
    pallas_call x0 -> x1, other arithmetic: none -> 1.88 us  [best_scores(): pl.pallas_call(_best_kernel, out_shape=jax.ShapeDtypeStruct((n, 1), jnp.f...]
    all_to_all x1, waiting for transfers between devices: 9.3 us -> 7.48 us  [per_device(): received = lax.all_to_all(local_best, 'cent', 0, 0, tiled=True)]
  transfers between devices with their start and end apart: 3 -> 3, of which waited for: 3 -> 3; matrix products, arithmetic and copies ran while one was open for 3% -> 5% of each run, Pallas kernels for 0% -> 0%
where the time goes in v8:
time: 171 us; the launch traced here: 170 us
  waiting for transfers between devices  85 us (50%)
  blocking collectives  23.1 us (14%)
  starting transfers between devices  22.7 us (13%)
  between operations  14.2 us (8%)
  local copies, waits for them, and re-layouts  11.5 us (7%)
  Pallas kernels  7.08 us (4%)
  other arithmetic  6.11 us (4%)
    all_gather x1, waiting for transfers between devices, per_device(): rows = lax.all_gather(points, 'cent', axis=0, tiled=True)  70.5 us
    all_gather x1, blocking collectives, per_device(): gathered = lax.all_gather(packed, 'dp', axis=0, tiled=True)  23.1 us
    all_to_all x1, starting transfers between devices, per_device(): lax.all_to_all(jnp.broadcast_to(assign[None], (ncent, pdev)), 'cent', 0,...  11.6 us
    all_to_all x1, starting transfers between devices, per_device(): received = lax.all_to_all(local_best, 'cent', 0, 0, tiled=True)  11.1 us
    all_to_all x1, waiting for transfers between devices, per_device(): received = lax.all_to_all(local_best, 'cent', 0, 0, tiled=True)  7.48 us
    pallas_call x1, Pallas kernels, best_scores(): pl.pallas_call(_best_kernel, out_shape=jax.ShapeDtypeStruct((n, 1), jnp.f...  7.08 us
    all_to_all x1, waiting for transfers between devices, per_device(): lax.all_to_all(jnp.broadcast_to(assign[None], (ncent, pdev)), 'cent', 0,...  6.25 us
    gather x1, local copies, waits for them, and re-layouts, per_device(): picked = jnp.take(rows, where, axis=0)  4.32 us
  transfers between devices with their start and end apart: 3, of which 3 were waited for; matrix products, arithmetic and copies ran while one was open for 5% of the time, Pallas kernels for 0%

profile of v8, /device:TPU:1, one launch (start us, length us, event | category | flops | bytes accessed | tf_op | source)
XLA Modules:
  0.0 170.4 jit_solution(13588455435821541586)
XLA Ops:
  7.2 0.0 all-gather.2.cloned.1.call-start
  7.2 0.7 all-gather.2.cloned.1.call-update
  7.9 1.3 broadcast_in_dim.32
  9.2 11.6 %all-to-all-start = ((s32[64,1,48]{2,1,0:T(1,128)}), s32[64,1,48]{2,1,0:T(1,128)S(1)}, u32[]{:S(2)}, u32[]{:S(2)}) async-start(s32[64,1,48]{2,1,0:T(1,128)} %broadcast_in_dim.32), calls=%async_computation | async-start | bytes 65536 | tf_op jit(solution)/shard_map/all_to_all | solution.py:43
  20.8 1.0 multiply_reduce_fusion.1
  21.8 0.0 copy-start
  21.8 1.9 %copy.28 = f32[512,1024]{0,1:T(8,128)S(1)} copy(f32[512,1024]{1,0:T(8,128)} %param.6) | data formatting | bytes 4194304 | tf_op args[2]
  23.8 0.0 copy-done
  23.8 6.2 %all-to-all-done = s32[64,1,48]{2,1,0:T(1,128)S(1)} async-done(((s32[64,1,48]{2,1,0:T(1,128)}), s32[64,1,48]{2,1,0:T(1,128)S(1)}, u32[]{:S(2)}, u32[]{:S(2)}) %all-to-all-start) | async-done | bytes 12320 | tf_op jit(solution)/shard_map/all_to_all | solution.py:43
  30.0 0.2 subtract_reduce_fusion
  30.2 0.1 reshape.214
  30.3 0.3 reduce-window.9
  30.6 0.1 slice.25
  30.7 0.1 sub.29
  30.8 0.1 slice_reduce_fusion
  30.9 0.1 add_bitcast_fusion
  31.0 0.2 select_reduce_fusion
  31.3 0.1 copy.29
  31.3 0.1 fusion.7
  31.5 0.8 gather_fusion.1
  32.3 0.1 copy.32
  32.4 70.5 %all-gather.2.cloned.1.call-done.rows_ref = bf16[3072,1024]{1,0:T(8,128)(2,1)} async-done(((bf16[48,1024]{1,0:T(8,128)(2,1)}), bf16[3072,1024]{1,0:T(8,128)(2,1)}) %all-gather.2.cloned.1.call-update) | async-done | bytes 6291472 | tf_op jit(solution)/shard_map/all_gather | solution.py:42
  102.9 4.3 %gather_fusion = bf16[48,1024]{1,0:T(8,128)(2,1)S(1)} fusion(bf16[3072,1024]{1,0:T(8,128)(2,1)} %all-gather.2.cloned.1.call-done.rows_ref, s32[1024]{0:T(1024)S(1)} %pad_clamp_fusion), kind=kCustom, calls=%fused_computation | custom fusion | bytes 196800 | tf_op jit(solution)/shard_map/jit(_take)/gather | solution.py:52
  107.3 0.1 broadcast_select_fusion
  107.4 0.1 concatenate.3
  107.5 23.1 %all_gather.7 = bf16[384,1152]{1,0:T(8,128)(2,1)S(1)} all-gather(bf16[48,1152]{1,0:T(8,128)(2,1)S(1)} %concatenate.3), channel_id=1, replica_groups=mesh['dp'=8,'cent'=64] {'dp'}, dimensions={0}, use_global_device_ids=true | all-gather | bytes 995328 | tf_op jit(solution)/shard_map/all_gather | solution.py:61
  130.5 0.2 add_reduce_fusion
  130.7 0.8 multiply_reduce_fusion
  131.6 1.3 convert_bitcast_fusion
  132.9 7.1 %shard_map.59 = f32[3072,1]{1,0:T(8,128)} custom-call(bf16[3072,1024]{1,0:T(8,128)(2,1)} %all-gather.2.cloned.1.call-done.rows_ref, bf16[1024,512]{1,0:T(8,128)(2,1)} %get-tuple-element.12.cent_t_ref), custom_call_target="tpu_custom_call" | custom-call | tf_op jit(solution)/shard_map/pallas_call | solution.py:19
  140.0 1.9 %reduce.5 = f32[3072]{0:T(1024)S(1)} reduce(f32[3072,1]{1,0:T(8,128)} %shard_map.59, f32[]{:T(128)} %constant.94), dimensions={1}, to_apply=%pallas_call.3.reduce_sub_computation | reduce | bytes 24580 | tf_op jit(solution)/shard_map/pallas_call | solution.py:19
  141.9 0.7 all_to_all.13
  142.6 11.1 %all-to-all-start.1 = ((f32[64,1,48]{2,1,0:T(1,128)}), f32[64,1,48]{2,1,0:T(1,128)S(1)}, u32[]{:S(2)}, u32[]{:S(2)}) async-start(f32[64,1,48]{2,1,0:T(1,128)} %bitcast.4), calls=%async_computation.1 | async-start | bytes 65536 | tf_op jit(solution)/shard_map/all_to_all | solution.py:70
  153.7 1.8 %copy.35 = f32[512,1024]{1,0:T(8,128)} copy(f32[512,1024]{0,1:T(8,128)S(1)} %get-tuple-element.13) | data formatting | bytes 4194304
  155.5 7.5 %all-to-all-done.1 = f32[64,1,48]{2,1,0:T(1,128)S(1)} async-done(((f32[64,1,48]{2,1,0:T(1,128)}), f32[64,1,48]{2,1,0:T(1,128)S(1)}, u32[]{:S(2)}, u32[]{:S(2)}) %all-to-all-start.1) | async-done | bytes 12320 | tf_op jit(solution)/shard_map/all_to_all | solution.py:70
  163.0 0.5 divide_reduce_fusion
  (9 shorter events, 0.1 us)
Async XLA Ops:
  7.2 95.8 %all-gather.2.cloned.1.call-start = ((), (), s32[]{:S(2)}) async-start(), calls=%async_computation.2 | async-start | bytes 6389760 | tf_op jit(solution)/shard_map/all_gather | solution.py:42
  9.2 20.9 %all-to-all-start = ((s32[64,1,48]{2,1,0:T(1,128)}), s32[64,1,48]{2,1,0:T(1,128)S(1)}, u32[]{:S(2)}, u32[]{:S(2)}) async-start(s32[64,1,48]{2,1,0:T(1,128)} %broadcast_in_dim.32), calls=%async_computation | async-start | bytes 65536 | tf_op jit(solution)/shard_map/all_to_all | solution.py:43
  21.8 2.0 %copy-start = (s32[512]{0:T(512)S(1)}, s32[512]{0:T(512)}, u32[]{:S(2)}) copy-start(s32[512]{0:T(512)} %param.7) | copy-start | bytes 6148
  142.6 20.4 %all-to-all-start.1 = ((f32[64,1,48]{2,1,0:T(1,128)}), f32[64,1,48]{2,1,0:T(1,128)S(1)}, u32[]{:S(2)}, u32[]{:S(2)}) async-start(f32[64,1,48]{2,1,0:T(1,128)} %bitcast.4), calls=%async_computation.1 | async-start | bytes 65536 | tf_op jit(solution)/shard_map/all_to_all | solution.py:70
Sparse Core Ops, SparseCore 0:
  11.3 91.5 all-gather.1
